TPU v7x, 512 devices: a whole 4x8x8 slice. The times are simulated.
512 devices in a mesh: dp: 16 (over z, core), expert: 32 (over x, y).
Axes of the slice: x: 4, y: 8, z: 8, core: 2. Of those that a mesh axis runs over, the one named last changes fastest.
Arguments:
- out_grad: bfloat16 [65536, 1024], P(('dp', 'expert')), may hold values from -6 to 6
- hidden: bfloat16 [65536, 8, 384], P(('dp', 'expert')), may hold values from -1.5 to 1.5
- gate: bfloat16 [65536, 8], P(('dp', 'expert')), may hold values from 0.049804688 to 0.5
- route_expert: int32 [65536, 8], P(('dp', 'expert')), may hold values from 0 to 63, as said below
- route_replica: int32 [65536, 8], P(('dp', 'expert')), may hold values from 0 to 3, as said below
- slot_expert: int32 [32, 3], replicated, may hold values from 0 to 63, as said below
- down_weight: bfloat16 [32, 3, 384, 1024], P('expert')
Outputs:
- d_hidden: bfloat16 [65536, 8, 384], P(('dp', 'expert'))
- d_gate: bfloat16 [65536, 8], P(('dp', 'expert'))
- d_weight: float32 [32, 3, 384, 1024], P('expert', None, 'dp')
Inputs may be any that keep to these rules, and one draw needn't show every extreme that they name: `slot_expert`: every expert holds 1 to 4 slots: exactly 8 experts hold 4, 8 hold 2, the rest 1. `route_expert`: the 8 experts of a token differ. Of the routes of one device's 128 tokens, at most 16 go to one slot, and some slot receives exactly 16 routes from every device. route_replica is below the number of slots of the route's expert.
All inputs are finite; a program needn't handle non-finite values.
Results may differ from a plain program's by a relative error of at most 0.0029.
Values may be sent and summed in bfloat16 or wider, within the bound.
No kernel may reach another device: no remote copies, remote signals or barrier semaphores. Data moves between devices by JAX's collectives and lax.ppermute only.
A program may use at most 128 MiB of HBM per device.

v0:
```python
import jax
import jax.numpy as jnp
from jax import lax
from jax.sharding import PartitionSpec as P

EXPERTS = 64
CAP = 16
HOT = 16


def slot_of_route(experts, replicas, flat_slots):
    slot_count = flat_slots.shape[0]
    ordering = jnp.arange(slot_count, dtype=jnp.int32)
    same_expert = flat_slots[:, None] == flat_slots[None, :]
    replica_rank = jnp.sum(
        (same_expert & (ordering[None, :] < ordering[:, None])).astype(jnp.int32), axis=1
    )
    matches = (experts.reshape(-1)[:, None] == flat_slots[None, :]) & (
        replicas.reshape(-1)[:, None] == replica_rank[None, :]
    )
    return jnp.sum(jnp.where(matches, ordering[None, :], 0), axis=1)


def buffer_places(experts, replicas, flat_slots, capacity):
    destination = slot_of_route(experts, replicas, flat_slots)
    slot_count = flat_slots.shape[0]
    onehot = (destination[:, None] == jnp.arange(slot_count, dtype=jnp.int32)[None, :]).astype(
        jnp.int32
    )
    before = jnp.cumsum(onehot, axis=0) - onehot
    position = jnp.sum(before * onehot, axis=1)
    return destination * capacity + position


def route_of_place(places, length):
    route_count = places.shape[0]
    return (
        jnp.full((length,), route_count, jnp.int32)
        .at[places]
        .set(jnp.arange(route_count, dtype=jnp.int32))
    )


def per_device(out_grad, hidden, gate, route_expert, route_replica, slot_expert, down_weight):
    tok_rows, chosen_count = gate.shape
    model_width = out_grad.shape[1]
    hidden_width = hidden.shape[2]
    groups, slots = slot_expert.shape
    flat_slots = slot_expert.reshape(-1)
    capacity = CAP
    block_rows = slots * capacity
    length = groups * block_rows
    route_count = tok_rows * chosen_count
    own_index = lax.axis_index("expert")
    places = buffer_places(route_expert, route_replica, flat_slots, capacity)
    source_route = route_of_place(places, length)
    hidden_rows = jnp.concatenate(
        [hidden.reshape(route_count, hidden_width), jnp.zeros((1, hidden_width), hidden.dtype)],
        axis=0,
    )
    gate_rows = jnp.concatenate([gate.reshape(route_count), jnp.zeros((1,), gate.dtype)])
    sent_hidden = hidden_rows[source_route].reshape(groups, block_rows, hidden_width)
    sent_gate = gate_rows[source_route].reshape(groups, block_rows)
    padded_grad = jnp.concatenate([out_grad, jnp.zeros((1, model_width), out_grad.dtype)], axis=0)
    token_rows = jnp.where(source_route < route_count, source_route // chosen_count, tok_rows)
    sent_grad = padded_grad[token_rows].reshape(groups, block_rows, model_width)
    got_grad, got_hidden, got_gate = (
        lax.all_to_all(sent_grad, "expert", split_axis=0, concat_axis=0, tiled=True),
        lax.all_to_all(sent_hidden, "expert", split_axis=0, concat_axis=0, tiled=True),
        lax.all_to_all(sent_gate, "expert", split_axis=0, concat_axis=0, tiled=True),
    )
    weights = down_weight[0]
    grad_four = got_grad.reshape(groups, slots, capacity, model_width)
    hidden_four = got_hidden.reshape(groups, slots, capacity, hidden_width)
    gate_four = got_gate.reshape(groups, slots, capacity).astype(jnp.float32)[..., None]
    projected = jnp.einsum("xscd,sfd->xscf", grad_four, weights, preferred_element_type=jnp.float32)
    back_rows = (
        (gate_four * projected).astype(jnp.bfloat16).reshape(groups, block_rows, hidden_width)
    )
    back_gate = (
        jnp.sum(hidden_four.astype(jnp.float32) * projected, axis=-1)
        .astype(jnp.bfloat16)
        .reshape(groups, block_rows)
    )
    came_rows, came_gate = (
        lax.all_to_all(back_rows, "expert", split_axis=0, concat_axis=0, tiled=True),
        lax.all_to_all(back_gate, "expert", split_axis=0, concat_axis=0, tiled=True),
    )
    d_hidden = came_rows.reshape(length, hidden_width)[places].reshape(
        tok_rows, chosen_count, hidden_width
    )
    d_gate = came_gate.reshape(length)[places].reshape(tok_rows, chosen_count)
    scaled = (gate_four * hidden_four.astype(jnp.float32)).astype(jnp.bfloat16)
    partial_value = jnp.einsum(
        "xscf,xscd->sfd", scaled, grad_four, preferred_element_type=jnp.float32
    )
    dp_count = lax.axis_size("dp")
    shares = lax.all_to_all(partial_value, "dp", split_axis=1, concat_axis=0, tiled=True)
    group_sum = jnp.sum(
        shares.reshape(dp_count, slots, hidden_width // dp_count, model_width), axis=0
    )
    own_slots = lax.dynamic_slice_in_dim(flat_slots, own_index * slots, slots)
    expert_ids = jnp.arange(EXPERTS, dtype=jnp.int32)
    copies = jnp.sum((flat_slots[:, None] == expert_ids[None, :]).astype(jnp.int32), axis=0)
    is_hot = copies >= 2
    hot_rank = jnp.cumsum(is_hot.astype(jnp.int32)) - 1
    picks = own_slots[:, None] == expert_ids[None, :]
    slot_hot = jnp.any(picks & is_hot[None, :], axis=1)
    slot_rank = jnp.sum(jnp.where(picks, hot_rank[None, :], 0), axis=1)
    member = (slot_rank[:, None] == jnp.arange(HOT, dtype=jnp.int32)[None, :]) & slot_hot[:, None]
    hot_table = jnp.sum(jnp.where(member[:, :, None, None], group_sum[:, None], 0.0), axis=0)
    hot_total = lax.psum(hot_table, "expert")
    from_table = jnp.sum(jnp.where(member[:, :, None, None], hot_total[None], 0.0), axis=1)
    d_weight = jnp.where(slot_hot[:, None, None], from_table, group_sum)[None]
    return (d_hidden, d_gate, d_weight)


def solution(mesh):
    placed = (
        P(("dp", "expert"), None),
        P(("dp", "expert"), None, None),
        P(("dp", "expert"), None),
        P(("dp", "expert"), None),
        P(("dp", "expert"), None),
        P(),
        P("expert", None, None, None),
    )
    return jax.shard_map(
        per_device,
        mesh=mesh,
        in_specs=placed,
        out_specs=(
            P(("dp", "expert"), None, None),
            P(("dp", "expert"), None),
            P("expert", None, "dp", None),
        ),
        check_vma=False,
    )
```

profile of v0, /device:TPU:8, one launch (start us, length us, event | category | flops | bytes accessed | tf_op | source)
XLA Modules:
  0.0 556.3 jit_solution(8288861238006414382)
XLA Ops:
  11.2 27.0 %reduce-window.18 = s32[96,8,128]{2,1,0:T(8,128)S(1)} reduce-window(s32[96,8,128]{2,1,0:T(8,128)S(1)} %fusion.14, s32[]{:T(128)} %constant.20.clone.1), window={size=1x1x128 pad=0_0x0_0x127_0}, to_apply=%region_2.3 | reduce-window | flops 12484608 | bytes 786436 | tf_op jit(solution)/shard_map/reduce-window
  39.6 4.3 scatter_custom_fusion
  44.0 9.5 %gather_fusion = bf16[1536]{0:T(1024)(128)(2,1)S(1)} fusion(bf16[1025]{0:T(1024)(128)(2,1)S(1)} %pad_maximum_fusion, s32[2048]{0:T(1024)S(1)} %get-tuple-element.28), kind=kCustom, calls=%fused_computation | custom fusion | bytes 12288 | tf_op jit(solution)/shard_map/gather | solution.py:63
  54.2 10.2 %all-to-all-start = ((bf16[32,1,48]{2,1,0:T(2,128)(2,1)}), bf16[32,1,48]{2,1,0:T(2,128)(2,1)S(1)}, u32[]{:S(2)}, u32[]{:S(2)}) async-start(bf16[32,1,48]{2,1,0:T(2,128)(2,1)} %all_to_all.36), calls=%async_computation | async-start | bytes 32768 | tf_op jit(solution)/shard_map/all_to_all | solution.py:70
  65.6 5.3 gather_fusion.3
  70.9 2.1 all-to-all-done
  72.9 7.9 %all-to-all-start.3 = ((bf16[32,48,384]{2,1,0:T(8,128)(2,1)}), bf16[32,48,384]{2,1,0:T(8,128)(2,1)}, u32[]{:S(2)}, u32[]{:S(2)}) async-start(bf16[32,48,384]{2,1,0:T(8,128)(2,1)} %bitcast.60), calls=%async_computation.3 | async-start | bytes 2359296 | tf_op jit(solution)/shard_map/all_to_all | solution.py:69
  80.9 5.8 %gather_fusion.1 = bf16[1536,1024]{1,0:T(8,128)(2,1)} fusion(bf16[129,1024]{1,0:T(8,128)(2,1)S(1)} %concatenate.10, s32[2048]{0:T(1024)S(1)} %get-tuple-element.27), kind=kCustom, calls=%fused_computation.1 | custom fusion | bytes 6297600 | tf_op jit(solution)/shard_map/gather | solution.py:66
  86.7 24.8 %all-to-all-done.3 = bf16[32,48,384]{2,1,0:T(8,128)(2,1)} async-done(((bf16[32,48,384]{2,1,0:T(8,128)(2,1)}), bf16[32,48,384]{2,1,0:T(8,128)(2,1)}, u32[]{:S(2)}, u32[]{:S(2)}) %all-to-all-start.3) | async-done | bytes 1179680 | tf_op jit(solution)/shard_map/all_to_all | solution.py:69
  111.5 5.4 all-to-all-start.1
  117.7 68.9 %all-to-all-done.1 = bf16[32,48,1024]{2,1,0:T(8,128)(2,1)} async-done(((bf16[32,48,1024]{2,1,0:T(8,128)(2,1)}), bf16[32,48,1024]{2,1,0:T(8,128)(2,1)}, u32[]{:S(2)}, u32[]{:S(2)}) %all-to-all-start.1) | async-done | bytes 3145760 | tf_op jit(solution)/shard_map/all_to_all | solution.py:68
  186.6 4.7 fusion.6
  192.9 9.7 %all-to-all-start.4 = ((bf16[32,1,48]{2,1,0:T(2,128)(2,1)}), bf16[32,1,48]{2,1,0:T(2,128)(2,1)S(1)}, u32[]{:S(2)}, u32[]{:S(2)}) async-start(bf16[32,1,48]{2,1,0:T(2,128)(2,1)} %copy.121), calls=%async_computation.4 | async-start | bytes 32768 | tf_op jit(solution)/shard_map/all_to_all | solution.py:87
  202.6 3.8 fusion.7
  206.4 5.9 %copy.125 = f32[3,384,1024]{2,0,1:T(4,128)} copy(f32[3,384,1024]{2,1,0:T(8,128)S(1)} %fusion.7) | data formatting | bytes 9437184 | tf_op jit(solution)/shard_map/xscf,xscd->sfd/dot_general | solution.py:94
  212.3 10.5 %all-to-all-start.5 = ((f32[3,384,1024]{2,0,1:T(4,128)}), f32[3,384,1024]{2,0,1:T(4,128)}, u32[]{:S(2)}, u32[]{:S(2)}) async-start(f32[3,384,1024]{2,0,1:T(4,128)} %copy.125), calls=%async_computation.5 | async-start | bytes 12582912 | tf_op jit(solution)/shard_map/all_to_all | solution.py:98
  229.3 132.7 %all-to-all-done.5 = f32[3,384,1024]{2,0,1:T(4,128)} async-done(((f32[3,384,1024]{2,0,1:T(4,128)}), f32[3,384,1024]{2,0,1:T(4,128)}, u32[]{:S(2)}, u32[]{:S(2)}) %all-to-all-start.5) | async-done | bytes 4718624 | tf_op jit(solution)/shard_map/all_to_all | solution.py:98
  362.0 9.8 %all-to-all-start.2 = ((bf16[32,48,384]{2,1,0:T(8,128)(2,1)}), bf16[32,48,384]{2,1,0:T(8,128)(2,1)S(1)}, u32[]{:S(2)}, u32[]{:S(2)}) async-start(bf16[32,48,384]{2,1,0:T(8,128)(2,1)} %bitcast.61), calls=%async_computation.2 | async-start | bytes 2359296 | tf_op jit(solution)/shard_map/all_to_all | solution.py:86
  375.6 5.3 reduce_sum.91
  382.1 2.5 select_reduce_fusion.1
  387.3 6.9 %gather_fusion.4 = bf16[1024]{0:T(1024)(128)(2,1)S(1)} fusion(bf16[1536]{0:T(1024)(128)(2,1)S(1)} %reshape.219, s32[1024]{0:T(1024)} %broadcast_clamp_fusion), kind=kCustom, calls=%fused_computation.4 | custom fusion | bytes 8192 | tf_op jit(solution)/shard_map/gather | solution.py:92
  396.4 6.4 %all-to-all-done.2 = bf16[32,48,384]{2,1,0:T(8,128)(2,1)S(1)} async-done(((bf16[32,48,384]{2,1,0:T(8,128)(2,1)}), bf16[32,48,384]{2,1,0:T(8,128)(2,1)S(1)}, u32[]{:S(2)}, u32[]{:S(2)}) %all-to-all-start.2) | async-done | bytes 1179680 | tf_op jit(solution)/shard_map/all_to_all | solution.py:86
  402.8 5.4 gather_fusion.2
  408.2 137.1 %all-reduce.4.cloned.1.call-done = f32[16,24,1024]{2,1,0:T(8,128)} async-done(((f32[16,24,1024]{2,1,0:T(8,128)}), f32[16,24,1024]{2,1,0:T(8,128)}) %all-reduce.4.cloned.1.call-update) | async-done | bytes 1572880 | tf_op jit(solution)/shard_map/psum | solution.py:112
  (67 shorter events, 30.1 us)
Async XLA Ops:
  7.2 179.5 %copy-start = (bf16[1,3,384,1024]{3,2,1,0:T(8,128)(2,1)S(1)}, bf16[1,3,384,1024]{3,2,1,0:T(8,128)(2,1)}, u32[]{:S(2)}) copy-start(bf16[1,3,384,1024]{3,2,1,0:T(8,128)(2,1)} %param.13) | copy-start | bytes 7077892
  10.9 27.4 %copy-start.3 = (s32[96]{0:T(128)}, s32[96]{0:T(128)S(1)}, u32[]{:S(2)}) copy-start(s32[96]{0:T(128)S(1)} %eq.109) | copy-start | bytes 1156
  39.1 0.6 copy-start.2
  54.2 18.7 %all-to-all-start = ((bf16[32,1,48]{2,1,0:T(2,128)(2,1)}), bf16[32,1,48]{2,1,0:T(2,128)(2,1)S(1)}, u32[]{:S(2)}, u32[]{:S(2)}) async-start(bf16[32,1,48]{2,1,0:T(2,128)(2,1)} %all_to_all.36), calls=%async_computation | async-start | bytes 32768 | tf_op jit(solution)/shard_map/all_to_all | solution.py:70
  70.9 10.0 %copy-start.1 = (bf16[128,1024]{1,0:T(8,128)(2,1)S(1)}, bf16[128,1024]{1,0:T(8,128)(2,1)}, u32[]{:S(2)}) copy-start(bf16[128,1024]{1,0:T(8,128)(2,1)} %param.7) | copy-start | bytes 786436
  72.9 38.6 %all-to-all-start.3 = ((bf16[32,48,384]{2,1,0:T(8,128)(2,1)}), bf16[32,48,384]{2,1,0:T(8,128)(2,1)}, u32[]{:S(2)}, u32[]{:S(2)}) async-start(bf16[32,48,384]{2,1,0:T(8,128)(2,1)} %bitcast.60), calls=%async_computation.3 | async-start | bytes 2359296 | tf_op jit(solution)/shard_map/all_to_all | solution.py:69
  111.5 75.1 %all-to-all-start.1 = ((bf16[32,48,1024]{2,1,0:T(8,128)(2,1)}), bf16[32,48,1024]{2,1,0:T(8,128)(2,1)}, u32[]{:S(2)}, u32[]{:S(2)}) async-start(bf16[32,48,1024]{2,1,0:T(8,128)(2,1)} %bitcast.59), calls=%async_computation.1 | async-start | bytes 6291456 | tf_op jit(solution)/shard_map/all_to_all | solution.py:68
  192.9 19.4 %all-to-all-start.4 = ((bf16[32,1,48]{2,1,0:T(2,128)(2,1)}), bf16[32,1,48]{2,1,0:T(2,128)(2,1)S(1)}, u32[]{:S(2)}, u32[]{:S(2)}) async-start(bf16[32,1,48]{2,1,0:T(2,128)(2,1)} %copy.121), calls=%async_computation.4 | async-start | bytes 32768 | tf_op jit(solution)/shard_map/all_to_all | solution.py:87
  212.3 149.7 %all-to-all-start.5 = ((f32[3,384,1024]{2,0,1:T(4,128)}), f32[3,384,1024]{2,0,1:T(4,128)}, u32[]{:S(2)}, u32[]{:S(2)}) async-start(f32[3,384,1024]{2,0,1:T(4,128)} %copy.125), calls=%async_computation.5 | async-start | bytes 12582912 | tf_op jit(solution)/shard_map/all_to_all | solution.py:98
  362.0 40.8 %all-to-all-start.2 = ((bf16[32,48,384]{2,1,0:T(8,128)(2,1)}), bf16[32,48,384]{2,1,0:T(8,128)(2,1)S(1)}, u32[]{:S(2)}, u32[]{:S(2)}) async-start(bf16[32,48,384]{2,1,0:T(8,128)(2,1)} %bitcast.61), calls=%async_computation.2 | async-start | bytes 2359296 | tf_op jit(solution)/shard_map/all_to_all | solution.py:86
  371.8 173.5 %all-reduce.4.cloned.1.call-start = ((), (), s32[]{:S(2)}) async-start(), calls=%async_computation.6 | async-start | bytes 3145728 | tf_op jit(solution)/shard_map/psum | solution.py:112
  374.4 0.6 copy-start.5
  402.8 142.5 %copy-start.4 = (pred[3,16]{1,0:T(4,128)(4,1)S(1)}, pred[3,16]{1,0:T(4,128)(4,1)}, u32[]{:S(2)}) copy-start(pred[3,16]{1,0:T(4,128)(4,1)} %fusion.23) | copy-start | bytes 148
  402.8 144.5 %copy-start.6 = (pred[3]{0:T(512)(128)(4,1)S(1)}, pred[3]{0:T(512)(128)(4,1)}, u32[]{:S(2)}) copy-start(pred[3]{0:T(512)(128)(4,1)} %copy-done.5) | copy-start | bytes 13
Sparse Core Ops, SparseCore 0:
  384.7 160.5 all-reduce.3
where the time goes:
time: 558 us; the launch traced here: 556 us
  waiting for transfers between devices  372 us (67%)
  local copies, waits for them, and re-layouts  61.4 us (11%)
  starting transfers between devices  53.5 us (10%)
  other arithmetic  46.5 us (8%)
  between operations  14.3 us (3%)
  matrix products  8.51 us (2%)
    psum x1, waiting for transfers between devices, per_device(): hot_total = lax.psum(hot_table, 'expert')  137 us
    all_to_all x1, waiting for transfers between devices, per_device(): lax.all_to_all(partial_value, 'dp', split_axis=1, concat_axis=0, tiled=True)  133 us
    all_to_all x1, waiting for transfers between devices, per_device(): lax.all_to_all(sent_grad, 'expert', split_axis=0, concat_axis=0, tiled=True)  68.9 us
    another operation x4, other arithmetic  28.7 us
    all_to_all x1, waiting for transfers between devices, per_device(): lax.all_to_all(sent_hidden, 'expert', split_axis=0, concat_axis=0, tiled=...  24.8 us
  transfers between devices with their start and end apart: 7, of which 6 were waited for; matrix products, arithmetic and copies ran while one was open for 11% of the time, Pallas kernels for 0%

commit v1 on v0

--- a/solution.py
+++ b/solution.py
@@ -24,11 +24,10 @@
 def buffer_places(experts, replicas, flat_slots, capacity):
     destination = slot_of_route(experts, replicas, flat_slots)
     slot_count = flat_slots.shape[0]
-    onehot = (destination[:, None] == jnp.arange(slot_count, dtype=jnp.int32)[None, :]).astype(
-        jnp.int32
-    )
-    before = jnp.cumsum(onehot, axis=0) - onehot
-    position = jnp.sum(before * onehot, axis=1)
+    route_count = destination.shape[0]
+    ordering = jnp.arange(route_count, dtype=jnp.int32)
+    earlier = (destination[:, None] == destination[None, :]) & (ordering[None, :] < ordering[:, None])
+    position = jnp.sum(earlier.astype(jnp.int32), axis=1)
     return destination * capacity + position
 
 
@@ -39,6 +38,14 @@
         .at[places]
         .set(jnp.arange(route_count, dtype=jnp.int32))
     )
+
+
+def exchange_sum(x, axis, count):
+    pieces = lax.all_to_all(x.reshape(count, -1), axis, split_axis=0, concat_axis=0, tiled=True)
+    own_total = jnp.sum(pieces, axis=0)
+    copies = jnp.broadcast_to(own_total[None], pieces.shape)
+    totals = lax.all_to_all(copies, axis, split_axis=0, concat_axis=0, tiled=True)
+    return totals.reshape(x.shape)
 
 
 def per_device(out_grad, hidden, gate, route_expert, route_replica, slot_expert, down_weight):
@@ -94,11 +101,7 @@
     partial_value = jnp.einsum(
         "xscf,xscd->sfd", scaled, grad_four, preferred_element_type=jnp.float32
     )
-    dp_count = lax.axis_size("dp")
-    shares = lax.all_to_all(partial_value, "dp", split_axis=1, concat_axis=0, tiled=True)
-    group_sum = jnp.sum(
-        shares.reshape(dp_count, slots, hidden_width // dp_count, model_width), axis=0
-    )
+    group_sum = lax.psum_scatter(partial_value, "dp", scatter_dimension=1, tiled=True)
     own_slots = lax.dynamic_slice_in_dim(flat_slots, own_index * slots, slots)
     expert_ids = jnp.arange(EXPERTS, dtype=jnp.int32)
     copies = jnp.sum((flat_slots[:, None] == expert_ids[None, :]).astype(jnp.int32), axis=0)
@@ -109,7 +112,7 @@
     slot_rank = jnp.sum(jnp.where(picks, hot_rank[None, :], 0), axis=1)
     member = (slot_rank[:, None] == jnp.arange(HOT, dtype=jnp.int32)[None, :]) & slot_hot[:, None]
     hot_table = jnp.sum(jnp.where(member[:, :, None, None], group_sum[:, None], 0.0), axis=0)
-    hot_total = lax.psum(hot_table, "expert")
+    hot_total = exchange_sum(hot_table, "expert", lax.axis_size("expert"))
     from_table = jnp.sum(jnp.where(member[:, :, None, None], hot_total[None], 0.0), axis=1)
     d_weight = jnp.where(slot_hot[:, None, None], from_table, group_sum)[None]
     return (d_hidden, d_gate, d_weight)

time: 558 us -> 393 us (0.70)
  the two profiles are of different devices: /device:TPU:8 before, /device:TPU:192 now
where the time goes in v1:
time: 393 us; the launch traced here: 391 us
  waiting for transfers between devices  238 us (61%)
  local copies, waits for them, and re-layouts  59.2 us (15%)
  starting transfers between devices  49.8 us (13%)
  other arithmetic  19.1 us (5%)
  between operations  14.3 us (4%)
  matrix products  10.6 us (3%)
    all_to_all x1, waiting for transfers between devices, per_device(): lax.all_to_all(sent_grad, 'expert', split_axis=0, concat_axis=0, tiled=True)  73.9 us
    reduce_scatter x1, waiting for transfers between devices, per_device(): lax.psum_scatter(partial_value, 'dp', scatter_dimension=1, tiled=True)  47.8 us
    all_to_all x1, waiting for transfers between devices, exchange_sum(): lax.all_to_all(x.reshape(count, -1), axis, split_axis=0, concat_axis=0, t...  36.8 us
    all_to_all x1, waiting for transfers between devices, per_device(): lax.all_to_all(back_rows, 'expert', split_axis=0, concat_axis=0, tiled=True)  29.1 us
    all_to_all x1, waiting for transfers between devices, per_device(): lax.all_to_all(sent_hidden, 'expert', split_axis=0, concat_axis=0, tiled=...  25.1 us
    all_to_all x1, waiting for transfers between devices, exchange_sum(): lax.all_to_all(copies, axis, split_axis=0, concat_axis=0, tiled=True)  22.3 us
    all_to_all x1, starting transfers between devices, per_device(): lax.all_to_all(sent_gate, 'expert', split_axis=0, concat_axis=0, tiled=True)  9.95 us
    gather x1, local copies, waits for them, and re-layouts, per_device(): sent_gate = gate_rows[source_route].reshape(groups, block_rows)  9.46 us
  transfers between devices with their start and end apart: 8, of which 7 were waited for; matrix products, arithmetic and copies ran while one was open for 11% of the time, Pallas kernels for 0%

profile of v1, /device:TPU:192, one launch (start us, length us, event | category | flops | bytes accessed | tf_op | source)
XLA Modules:
  0.0 391.3 jit_solution(9448544761075823984)
XLA Ops:
  10.9 4.3 %scatter_custom_fusion = s32[1536]{0:T(1024)S(1)} fusion(s32[1024]{0:T(1024)S(1)} %bitcast.45, s32[1024]{0:T(1024)S(1)} %iota.30, s32[]{:T(128)} %constant.19.clone.1), kind=kCustom, calls=%fused_computation.46 | custom fusion | bytes 6148 | tf_op jit(solution)/shard_map/scatter | solution.py:39
  16.2 9.5 %gather_fusion = bf16[1536]{0:T(1024)(128)(2,1)S(1)} fusion(bf16[1025]{0:T(1024)(128)(2,1)S(1)} %pad_maximum_fusion, s32[2048]{0:T(1024)S(1)} %get-tuple-element.25), kind=kCustom, calls=%fused_computation | custom fusion | bytes 12288 | tf_op jit(solution)/shard_map/gather | solution.py:70
  26.3 9.9 %all-to-all-start = ((bf16[32,1,48]{2,1,0:T(2,128)(2,1)}), bf16[32,1,48]{2,1,0:T(2,128)(2,1)S(1)}, u32[]{:S(2)}, u32[]{:S(2)}) async-start(bf16[32,1,48]{2,1,0:T(2,128)(2,1)} %all_to_all.38), calls=%async_computation | async-start | bytes 32768 | tf_op jit(solution)/shard_map/all_to_all | solution.py:77
  37.5 5.3 %gather_fusion.3 = bf16[1536,384]{1,0:T(8,128)(2,1)} fusion(bf16[1025,384]{1,0:T(8,128)(2,1)S(1)} %concatenate.11, s32[2048]{0:T(1024)S(1)} %get-tuple-element.25), kind=kCustom, calls=%fused_computation.3 | custom fusion | bytes 2365440 | tf_op jit(solution)/shard_map/gather | solution.py:69
  46.0 6.8 %all-to-all-start.3 = ((bf16[32,48,384]{2,1,0:T(8,128)(2,1)}), bf16[32,48,384]{2,1,0:T(8,128)(2,1)}, u32[]{:S(2)}, u32[]{:S(2)}) async-start(bf16[32,48,384]{2,1,0:T(8,128)(2,1)} %bitcast.38), calls=%async_computation.3 | async-start | bytes 2359296 | tf_op jit(solution)/shard_map/all_to_all | solution.py:76
  52.9 5.8 %gather_fusion.1 = bf16[1536,1024]{1,0:T(8,128)(2,1)} fusion(bf16[129,1024]{1,0:T(8,128)(2,1)S(1)} %concatenate.10, s32[2048]{0:T(1024)S(1)} %get-tuple-element.24), kind=kCustom, calls=%fused_computation.1 | custom fusion | bytes 6297600 | tf_op jit(solution)/shard_map/gather | solution.py:73
  58.7 25.1 %all-to-all-done.3 = bf16[32,48,384]{2,1,0:T(8,128)(2,1)} async-done(((bf16[32,48,384]{2,1,0:T(8,128)(2,1)}), bf16[32,48,384]{2,1,0:T(8,128)(2,1)}, u32[]{:S(2)}, u32[]{:S(2)}) %all-to-all-start.3) | async-done | bytes 1179680 | tf_op jit(solution)/shard_map/all_to_all | solution.py:76
  83.8 5.1 %all-to-all-start.1 = ((bf16[32,48,1024]{2,1,0:T(8,128)(2,1)}), bf16[32,48,1024]{2,1,0:T(8,128)(2,1)}, u32[]{:S(2)}, u32[]{:S(2)}) async-start(bf16[32,48,1024]{2,1,0:T(8,128)(2,1)} %bitcast.37), calls=%async_computation.1 | async-start | bytes 6291456 | tf_op jit(solution)/shard_map/all_to_all | solution.py:75
  89.1 73.9 %all-to-all-done.1 = bf16[32,48,1024]{2,1,0:T(8,128)(2,1)} async-done(((bf16[32,48,1024]{2,1,0:T(8,128)(2,1)}), bf16[32,48,1024]{2,1,0:T(8,128)(2,1)}, u32[]{:S(2)}, u32[]{:S(2)}) %all-to-all-start.1) | async-done | bytes 3145760 | tf_op jit(solution)/shard_map/all_to_all | solution.py:75
  163.0 5.9 %fusion.8 = f32[3,384,1024]{2,1,0:T(8,128)} fusion(bf16[32,3,16,1024]{3,2,1,0:T(8,128)(2,1)} %bitcast.4, f32[32,3,16]{2,0,1:T(8,128)S(1)} %copy.81, bf16[32,3,16,384]{3,2,1,0:T(8,128)(2,1)} %bitcast.17), kind=kOutput, calls=%fused_computation.21 | convolution fusion | flops 1209729024 | bytes 9050112 | tf_op jit(solution)/shard_map/xscf,xscd->sfd/dot_general | solution.py:101
  170.9 4.7 %fusion.7 = (bf16[32,3,16]{2,0,1:T(8,128)(2,1)}, bf16[32,3,16,384]{3,2,0,1:T(8,128)(2,1)S(1)}) fusion(f32[32,3,16]{2,0,1:T(8,128)} %copy-done.3, bf16[1,3,384,1024]{3,2,1,0:T(8,128)(2,1)S(1)} %copy-done, bf16[32,3,16,1024]{3,2,1,0:T(8,128)(2,1)} %bitcast.4, bf16[32,3,16,384]{3,2,1,0:T(8,128)(2,1)} %bitcast.17), kind=kOutput, calls=%fused_computation.19 | convolution fusion | flops 1210907136 | bytes 7873536 | tf_op jit(solution)/shard_map/xscd,sfd->xscf/dot_general | solution.py:83
  177.1 5.4 %all-to-all-start.4 = ((bf16[32,1,48]{2,1,0:T(2,128)(2,1)}), bf16[32,1,48]{2,1,0:T(2,128)(2,1)S(1)}, u32[]{:S(2)}, u32[]{:S(2)}) async-start(bf16[32,1,48]{2,1,0:T(2,128)(2,1)} %copy.86), calls=%async_computation.4 | async-start | bytes 32768 | tf_op jit(solution)/shard_map/all_to_all | solution.py:94
  182.6 47.8 %reduce-scatter.2.cloned.1.call-done = f32[3,24,1024]{2,1,0:T(8,128)} async-done(((f32[3,384,1024]{2,1,0:T(8,128)}), f32[3,24,1024]{2,1,0:T(8,128)}) %reduce-scatter.2.cloned.1.call-update) | async-done | bytes 294928 | tf_op jit(solution)/shard_map/reduce_scatter | solution.py:104
  233.2 4.0 %all_to_all.39 = f32[32,1,12288]{2,1,0:T(1,128)} reshape(f32[16,24,1024]{2,1,0:T(8,128)} %select_reduce_fusion.1) | data formatting | bytes 3145728 | tf_op jit(solution)/shard_map/all_to_all | solution.py:44
  237.2 9.4 %all-to-all-start.5 = ((f32[32,1,12288]{2,1,0:T(1,128)}), f32[32,1,12288]{2,1,0:T(1,128)}, u32[]{:S(2)}, u32[]{:S(2)}) async-start(f32[32,1,12288]{2,1,0:T(1,128)} %all_to_all.39), calls=%async_computation.6 | async-start | bytes 3145728 | tf_op jit(solution)/shard_map/all_to_all | solution.py:44
  247.7 36.8 %all-to-all-done.5 = f32[32,1,12288]{2,1,0:T(1,128)} async-done(((f32[32,1,12288]{2,1,0:T(1,128)}), f32[32,1,12288]{2,1,0:T(1,128)}, u32[]{:S(2)}, u32[]{:S(2)}) %all-to-all-start.5) | async-done | bytes 1572896 | tf_op jit(solution)/shard_map/all_to_all | solution.py:44
  284.6 7.3 %all-to-all-start.2 = ((bf16[32,48,384]{2,1,0:T(8,128)(2,1)}), bf16[32,48,384]{2,1,0:T(8,128)(2,1)S(1)}, u32[]{:S(2)}, u32[]{:S(2)}) async-start(bf16[32,48,384]{2,1,0:T(8,128)(2,1)} %bitcast.39), calls=%async_computation.2 | async-start | bytes 2359296 | tf_op jit(solution)/shard_map/all_to_all | solution.py:93
  294.9 29.1 %all-to-all-done.2 = bf16[32,48,384]{2,1,0:T(8,128)(2,1)S(1)} async-done(((bf16[32,48,384]{2,1,0:T(8,128)(2,1)}), bf16[32,48,384]{2,1,0:T(8,128)(2,1)S(1)}, u32[]{:S(2)}, u32[]{:S(2)}) %all-to-all-start.2) | async-done | bytes 1179680 | tf_op jit(solution)/shard_map/all_to_all | solution.py:93
  324.0 3.4 broadcast_in_dim.127
  327.3 5.8 %all-to-all-start.6 = ((f32[32,1,12288]{2,1,0:T(1,128)}), f32[32,1,12288]{2,1,0:T(1,128)}, u32[]{:S(2)}, u32[]{:S(2)}) async-start(f32[32,1,12288]{2,1,0:T(1,128)} %broadcast_in_dim.127), calls=%async_computation.7 | async-start | bytes 3145728 | tf_op jit(solution)/shard_map/all_to_all | solution.py:47
  335.9 6.9 %gather_fusion.4 = bf16[1024]{0:T(1024)(128)(2,1)S(1)} fusion(bf16[1536]{0:T(1024)(128)(2,1)S(1)} %reshape.202, s32[1024]{0:T(1024)} %broadcast_clamp_fusion), kind=kCustom, calls=%fused_computation.4 | custom fusion | bytes 8192 | tf_op jit(solution)/shard_map/gather | solution.py:99
  345.0 5.3 %gather_fusion.2 = bf16[1024,384]{1,0:T(8,128)(2,1)} fusion(bf16[1536,384]{1,0:T(8,128)(2,1)S(1)} %bitcast.36, s32[1024]{0:T(1024)} %broadcast_clamp_fusion), kind=kCustom, calls=%fused_computation.2 | custom fusion | bytes 1576960 | tf_op jit(solution)/shard_map/gather | solution.py:96
  350.2 22.3 %all-to-all-done.6 = f32[32,1,12288]{2,1,0:T(1,128)} async-done(((f32[32,1,12288]{2,1,0:T(1,128)}), f32[32,1,12288]{2,1,0:T(1,128)}, u32[]{:S(2)}, u32[]{:S(2)}) %all-to-all-start.6) | async-done | bytes 1572896 | tf_op jit(solution)/shard_map/all_to_all | solution.py:47
  372.6 6.3 %reduce.3 = f32[32,12288]{1,0:T(8,128)} reduce(f32[32,1,12288]{2,1,0:T(1,128)} %all-to-all-done.6, f32[]{:T(128)} %constant.66), dimensions={1}, to_apply=%all_to_all.37.reduce_sub_computation | reduce | bytes 3145732 | tf_op jit(solution)/shard_map/all_to_all | solution.py:47
  (64 shorter events, 30.9 us)
Async XLA Ops:
  7.2 163.7 %copy-start = (bf16[1,3,384,1024]{3,2,1,0:T(8,128)(2,1)S(1)}, bf16[1,3,384,1024]{3,2,1,0:T(8,128)(2,1)}, u32[]{:S(2)}) copy-start(bf16[1,3,384,1024]{3,2,1,0:T(8,128)(2,1)} %param.13) | copy-start | bytes 7077892
  10.8 4.3 %copy-start.4 = (s32[1024,1]{0,1:T(1,128)}, s32[1024,1]{0,1:T(1,128)S(1)}, u32[]{:S(2)}) copy-start(s32[1024,1]{0,1:T(1,128)S(1)} %compare_select_fusion) | copy-start | bytes 12292
  26.3 19.7 %all-to-all-start = ((bf16[32,1,48]{2,1,0:T(2,128)(2,1)}), bf16[32,1,48]{2,1,0:T(2,128)(2,1)S(1)}, u32[]{:S(2)}, u32[]{:S(2)}) async-start(bf16[32,1,48]{2,1,0:T(2,128)(2,1)} %all_to_all.38), calls=%async_computation | async-start | bytes 32768 | tf_op jit(solution)/shard_map/all_to_all | solution.py:77
  42.8 10.0 %copy-start.2 = (bf16[128,1024]{1,0:T(8,128)(2,1)S(1)}, bf16[128,1024]{1,0:T(8,128)(2,1)}, u32[]{:S(2)}) copy-start(bf16[128,1024]{1,0:T(8,128)(2,1)} %param.7) | copy-start | bytes 786436
  46.0 37.8 %all-to-all-start.3 = ((bf16[32,48,384]{2,1,0:T(8,128)(2,1)}), bf16[32,48,384]{2,1,0:T(8,128)(2,1)}, u32[]{:S(2)}, u32[]{:S(2)}) async-start(bf16[32,48,384]{2,1,0:T(8,128)(2,1)} %bitcast.38), calls=%async_computation.3 | async-start | bytes 2359296 | tf_op jit(solution)/shard_map/all_to_all | solution.py:76
  83.8 79.2 %all-to-all-start.1 = ((bf16[32,48,1024]{2,1,0:T(8,128)(2,1)}), bf16[32,48,1024]{2,1,0:T(8,128)(2,1)}, u32[]{:S(2)}, u32[]{:S(2)}) async-start(bf16[32,48,1024]{2,1,0:T(8,128)(2,1)} %bitcast.37), calls=%async_computation.1 | async-start | bytes 6291456 | tf_op jit(solution)/shard_map/all_to_all | solution.py:75
  88.9 141.5 %reduce-scatter.2.cloned.1.call-start = ((), (), s32[]{:S(2)}) async-start(), calls=%async_computation.8 | async-start | bytes 5013504 | tf_op jit(solution)/shard_map/reduce_scatter | solution.py:104
  89.1 79.8 %copy-start.3 = (f32[32,3,16]{2,0,1:T(8,128)}, f32[32,3,16]{2,0,1:T(8,128)S(1)}, u32[]{:S(2)}) copy-start(f32[32,3,16]{2,0,1:T(8,128)S(1)} %copy.81) | copy-start | bytes 18436
  169.6 0.6 copy-start.6
  177.1 60.1 %all-to-all-start.4 = ((bf16[32,1,48]{2,1,0:T(2,128)(2,1)}), bf16[32,1,48]{2,1,0:T(2,128)(2,1)S(1)}, u32[]{:S(2)}, u32[]{:S(2)}) async-start(bf16[32,1,48]{2,1,0:T(2,128)(2,1)} %copy.86), calls=%async_computation.4 | async-start | bytes 32768 | tf_op jit(solution)/shard_map/all_to_all | solution.py:94
  237.2 47.4 %all-to-all-start.5 = ((f32[32,1,12288]{2,1,0:T(1,128)}), f32[32,1,12288]{2,1,0:T(1,128)}, u32[]{:S(2)}, u32[]{:S(2)}) async-start(f32[32,1,12288]{2,1,0:T(1,128)} %all_to_all.39), calls=%async_computation.6 | async-start | bytes 3145728 | tf_op jit(solution)/shard_map/all_to_all | solution.py:44
  284.6 39.4 %all-to-all-start.2 = ((bf16[32,48,384]{2,1,0:T(8,128)(2,1)}), bf16[32,48,384]{2,1,0:T(8,128)(2,1)S(1)}, u32[]{:S(2)}, u32[]{:S(2)}) async-start(bf16[32,48,384]{2,1,0:T(8,128)(2,1)} %bitcast.39), calls=%async_computation.2 | async-start | bytes 2359296 | tf_op jit(solution)/shard_map/all_to_all | solution.py:93
  327.3 45.2 %all-to-all-start.6 = ((f32[32,1,12288]{2,1,0:T(1,128)}), f32[32,1,12288]{2,1,0:T(1,128)}, u32[]{:S(2)}, u32[]{:S(2)}) async-start(f32[32,1,12288]{2,1,0:T(1,128)} %broadcast_in_dim.127), calls=%async_computation.7 | async-start | bytes 3145728 | tf_op jit(solution)/shard_map/all_to_all | solution.py:47
  378.9 2.8 copy-start.5
  378.9 4.8 %copy-start.1 = (f32[3,24,1024]{2,1,0:T(8,128)S(1)}, f32[3,24,1024]{2,1,0:T(8,128)}, u32[]{:S(2)}) copy-start(f32[3,24,1024]{2,1,0:T(8,128)} %reduce-scatter.2.cloned.1.call-done) | copy-start | bytes 884740
  378.9 4.8 %copy-start.7 = (pred[3]{0:T(512)(128)(4,1)S(1)}, pred[3]{0:T(512)(128)(4,1)}, u32[]{:S(2)}) copy-start(pred[3]{0:T(512)(128)(4,1)} %copy-done.6) | copy-start | bytes 13
Sparse Core Ops, SparseCore 0:
  169.0 61.2 reduce-scatter.1

commit v2 on v1

--- a/solution.py
+++ b/solution.py
@@ -23,7 +23,6 @@
 
 def buffer_places(experts, replicas, flat_slots, capacity):
     destination = slot_of_route(experts, replicas, flat_slots)
-    slot_count = flat_slots.shape[0]
     route_count = destination.shape[0]
     ordering = jnp.arange(route_count, dtype=jnp.int32)
     earlier = (destination[:, None] == destination[None, :]) & (ordering[None, :] < ordering[:, None])
@@ -71,11 +70,13 @@
     padded_grad = jnp.concatenate([out_grad, jnp.zeros((1, model_width), out_grad.dtype)], axis=0)
     token_rows = jnp.where(source_route < route_count, source_route // chosen_count, tok_rows)
     sent_grad = padded_grad[token_rows].reshape(groups, block_rows, model_width)
-    got_grad, got_hidden, got_gate = (
-        lax.all_to_all(sent_grad, "expert", split_axis=0, concat_axis=0, tiled=True),
-        lax.all_to_all(sent_hidden, "expert", split_axis=0, concat_axis=0, tiled=True),
-        lax.all_to_all(sent_gate, "expert", split_axis=0, concat_axis=0, tiled=True),
-    )
+    lane = 128
+    gate_block = jnp.pad(sent_gate[..., None], ((0, 0), (0, 0), (0, lane - 1)))
+    sent = jnp.concatenate([sent_grad, sent_hidden, gate_block], axis=-1)
+    got = lax.all_to_all(sent, "expert", split_axis=0, concat_axis=0, tiled=True)
+    got_grad = got[..., :model_width]
+    got_hidden = got[..., model_width : model_width + hidden_width]
+    got_gate = got[..., model_width + hidden_width]
     weights = down_weight[0]
     grad_four = got_grad.reshape(groups, slots, capacity, model_width)
     hidden_four = got_hidden.reshape(groups, slots, capacity, hidden_width)
@@ -89,10 +90,16 @@
         .astype(jnp.bfloat16)
         .reshape(groups, block_rows)
     )
-    came_rows, came_gate = (
-        lax.all_to_all(back_rows, "expert", split_axis=0, concat_axis=0, tiled=True),
-        lax.all_to_all(back_gate, "expert", split_axis=0, concat_axis=0, tiled=True),
+    back_block = jnp.pad(back_gate[..., None], ((0, 0), (0, 0), (0, lane - 1)))
+    came = lax.all_to_all(
+        jnp.concatenate([back_rows, back_block], axis=-1),
+        "expert",
+        split_axis=0,
+        concat_axis=0,
+        tiled=True,
     )
+    came_rows = came[..., :hidden_width]
+    came_gate = came[..., hidden_width]
     d_hidden = came_rows.reshape(length, hidden_width)[places].reshape(
         tok_rows, chosen_count, hidden_width
     )

time: 393 us -> 401 us (1.020)
  blocking collectives: 0 us -> 116 us
  waiting for transfers between devices: 238 us -> 147 us
  starting transfers between devices: 49.8 us -> 23.9 us
  local copies, waits for them, and re-layouts: 59.2 us -> 66.2 us
  other arithmetic: 19.1 us -> 24.2 us
    all_to_all x0 -> x1, blocking collectives: none -> 116 us  [per_device(): lax.all_to_all(sent, 'expert', split_axis=0, concat_axis=0, tiled=True)]
    all_to_all x5 -> x1, waiting for transfers between devices: 131 us -> 37.6 us  [per_device(): lax.all_to_all(jnp.concatenate([back_rows, back_block], axis=-1), 'expert...]
    all_to_all x5 -> x1, starting transfers between devices: 34.5 us -> 7.69 us  [per_device(): lax.all_to_all(jnp.concatenate([back_rows, back_block], axis=-1), 'expert...]
    reduce_scatter x1, waiting for transfers between devices: 47.8 us -> 56.9 us  [per_device(): lax.psum_scatter(partial_value, 'dp', scatter_dimension=1, tiled=True)]
    all_to_all x1, waiting for transfers between devices: 36.8 us -> 28.7 us  [exchange_sum(): lax.all_to_all(x.reshape(count, -1), axis, split_axis=0, concat_axis=0, t...]
    slice x0 -> x5, local copies, waits for them, and re-layouts: none -> 7.47 us  [the longest x1 2.37 us: per_device(): got_grad = got[..., :model_width]]
    concatenate x0 -> x2, other arithmetic: none -> 4.9 us  [the longest x1 2.52 us: per_device(): sent = jnp.concatenate([sent_grad, sent_hidden, gate_block], axis=-1)]
  transfers between devices with their start and end apart: 8 -> 4, of which waited for: 7 -> 4; matrix products, arithmetic and copies ran while one was open for 11% -> 8% of each run, Pallas kernels for 0% -> 0%
where the time goes in v2:
time: 401 us; the launch traced here: 400 us
  waiting for transfers between devices  147 us (37%)
  blocking collectives  116 us (29%)
  local copies, waits for them, and re-layouts  66.2 us (17%)
  other arithmetic  24.2 us (6%)
  starting transfers between devices  23.9 us (6%)
  between operations  14.3 us (4%)
  matrix products  8.02 us (2%)
    all_to_all x1, blocking collectives, per_device(): lax.all_to_all(sent, 'expert', split_axis=0, concat_axis=0, tiled=True)  116 us
    reduce_scatter x1, waiting for transfers between devices, per_device(): lax.psum_scatter(partial_value, 'dp', scatter_dimension=1, tiled=True)  56.9 us
    all_to_all x1, waiting for transfers between devices, per_device(): lax.all_to_all(jnp.concatenate([back_rows, back_block], axis=-1), 'expert...  37.6 us
    all_to_all x1, waiting for transfers between devices, exchange_sum(): lax.all_to_all(x.reshape(count, -1), axis, split_axis=0, concat_axis=0, t...  28.7 us
    all_to_all x1, waiting for transfers between devices, exchange_sum(): lax.all_to_all(copies, axis, split_axis=0, concat_axis=0, tiled=True)  24.2 us
    all_to_all x1, starting transfers between devices, exchange_sum(): lax.all_to_all(x.reshape(count, -1), axis, split_axis=0, concat_axis=0, t...  9.84 us
    gather x1, local copies, waits for them, and re-layouts, per_device(): sent_gate = gate_rows[source_route].reshape(groups, block_rows)  9.46 us
  transfers between devices with their start and end apart: 4, of which 4 were waited for; matrix products, arithmetic and copies ran while one was open for 8% of the time, Pallas kernels for 0%

profile of v2, /device:TPU:192, one launch (start us, length us, event | category | flops | bytes accessed | tf_op | source)
XLA Modules:
  0.0 400.3 jit_solution(4201051943626933277)
XLA Ops:
  10.9 4.3 %scatter_custom_fusion = s32[1536]{0:T(1024)S(1)} fusion(s32[1024]{0:T(1024)S(1)} %bitcast.49, s32[1024]{0:T(1024)S(1)} %iota.30, s32[]{:T(128)} %constant.19.clone.1), kind=kCustom, calls=%fused_computation.53 | custom fusion | bytes 6148 | tf_op jit(solution)/shard_map/scatter | solution.py:38
  17.4 5.3 %gather_fusion.1 = bf16[1536,384]{1,0:T(8,128)(2,1)} fusion(bf16[1025,384]{1,0:T(8,128)(2,1)S(1)} %concatenate.16, s32[2048]{0:T(1024)S(1)} %get-tuple-element.21), kind=kCustom, calls=%fused_computation.1 | custom fusion | bytes 2365440 | tf_op jit(solution)/shard_map/gather | solution.py:68
  22.7 9.5 %gather_fusion.2 = bf16[1536]{0:T(1024)(128)(2,1)S(1)} fusion(bf16[1025]{0:T(1024)(128)(2,1)S(1)} %pad_maximum_fusion, s32[2048]{0:T(1024)S(1)} %get-tuple-element.21), kind=kCustom, calls=%fused_computation.2 | custom fusion | bytes 12288 | tf_op jit(solution)/shard_map/gather | solution.py:69
  32.9 5.8 %gather_fusion = bf16[1536,1024]{1,0:T(8,128)(2,1)} fusion(bf16[129,1024]{1,0:T(8,128)(2,1)S(1)} %concatenate.15, s32[2048]{0:T(1024)S(1)} %get-tuple-element.22), kind=kCustom, calls=%fused_computation | custom fusion | bytes 6297600 | tf_op jit(solution)/shard_map/gather | solution.py:72
  38.7 2.5 fusion.1
  41.3 116.3 %all_to_all.26 = bf16[32,48,1536]{2,1,0:T(8,128)(2,1)S(1)} all-to-all(bf16[32,48,1536]{2,1,0:T(8,128)(2,1)S(1)} %fusion.1), channel_id=1, replica_groups=mesh['dp'=16,'expert'=32] {'expert'}, dimensions={0} | all-to-all | bytes 9437184 | tf_op jit(solution)/shard_map/all_to_all | solution.py:76
  165.6 3.6 fusion.11
  174.1 56.9 %reduce-scatter.2.cloned.1.call-done = f32[3,24,1024]{2,1,0:T(8,128)} async-done(((f32[3,384,1024]{2,1,0:T(8,128)}), f32[3,24,1024]{2,1,0:T(8,128)}) %reduce-scatter.2.cloned.1.call-update) | async-done | bytes 294928 | tf_op jit(solution)/shard_map/reduce_scatter | solution.py:111
  231.0 2.9 select_reduce_fusion.1
  233.9 4.0 all_to_all.21
  237.8 9.8 %all-to-all-start.2 = ((f32[32,1,12288]{2,1,0:T(1,128)}), f32[32,1,12288]{2,1,0:T(1,128)}, u32[]{:S(2)}, u32[]{:S(2)}) async-start(f32[32,1,12288]{2,1,0:T(1,128)} %all_to_all.21), calls=%async_computation.3 | async-start | bytes 3145728 | tf_op jit(solution)/shard_map/all_to_all | solution.py:43
  247.7 4.4 %fusion.9 = (bf16[32,3,16,384]{3,2,0,1:T(8,128)(2,1)S(1)}, bf16[32,3,16]{2,0,1:T(8,128)(2,1)}) fusion(f32[32,3,16]{2,0,1:T(8,128)} %copy.72, bf16[1,3,384,1024]{3,2,1,0:T(8,128)(2,1)S(1)} %copy-done, bf16[32,3,16,1024]{3,2,1,0:T(8,128)(2,1)} %bitcast.41, bf16[32,3,16,384]{3,2,1,0:T(8,128)(2,1)S(1)} %bitcast.43), kind=kOutput, calls=%fused_computation.23 | convolution fusion | flops 1210907136 | bytes 7873536 | tf_op jit(solution)/shard_map/xscd,sfd->xscf/dot_general | solution.py:84
  254.2 2.4 fusion.14
  256.6 28.7 %all-to-all-done.2 = f32[32,1,12288]{2,1,0:T(1,128)} async-done(((f32[32,1,12288]{2,1,0:T(1,128)}), f32[32,1,12288]{2,1,0:T(1,128)}, u32[]{:S(2)}, u32[]{:S(2)}) %all-to-all-start.2) | async-done | bytes 1572896 | tf_op jit(solution)/shard_map/all_to_all | solution.py:43
  285.3 7.7 %all-to-all-start.1 = ((bf16[32,48,512]{2,1,0:T(8,128)(2,1)}), bf16[32,48,512]{2,1,0:T(8,128)(2,1)}, u32[]{:S(2)}, u32[]{:S(2)}) async-start(bf16[32,48,512]{2,1,0:T(8,128)(2,1)} %fusion.14), calls=%async_computation.1 | async-start | bytes 3145728 | tf_op jit(solution)/shard_map/all_to_all | solution.py:94
  293.0 2.4 reduce_sum.88
  295.4 37.6 %all-to-all-done.1 = bf16[32,48,512]{2,1,0:T(8,128)(2,1)} async-done(((bf16[32,48,512]{2,1,0:T(8,128)(2,1)}), bf16[32,48,512]{2,1,0:T(8,128)(2,1)}, u32[]{:S(2)}, u32[]{:S(2)}) %all-to-all-start.1) | async-done | bytes 1572896 | tf_op jit(solution)/shard_map/all_to_all | solution.py:94
  333.0 2.6 broadcast_in_dim.127
  335.6 6.4 %all-to-all-start.3 = ((f32[32,1,12288]{2,1,0:T(1,128)}), f32[32,1,12288]{2,1,0:T(1,128)}, u32[]{:S(2)}, u32[]{:S(2)}) async-start(f32[32,1,12288]{2,1,0:T(1,128)} %broadcast_in_dim.127), calls=%async_computation.4 | async-start | bytes 3145728 | tf_op jit(solution)/shard_map/all_to_all | solution.py:46
  344.8 5.0 %gather_fusion.3 = bf16[1024,384]{1,0:T(8,128)(2,1)} fusion(bf16[1536,384]{1,0:T(8,128)(2,1)S(1)} %bitcast.36, s32[1024]{0:T(1024)S(1)} %broadcast_clamp_fusion), kind=kCustom, calls=%fused_computation.3 | custom fusion | bytes 1576960 | tf_op jit(solution)/shard_map/gather | solution.py:103
  349.8 6.8 %gather_fusion.4 = bf16[1024]{0:T(1024)(128)(2,1)S(1)} fusion(bf16[1536]{0:T(1024)(128)(2,1)S(1)} %reshape_squeeze.4, s32[1024]{0:T(1024)S(1)} %broadcast_clamp_fusion), kind=kCustom, calls=%fused_computation.4 | custom fusion | bytes 8192 | tf_op jit(solution)/shard_map/gather | solution.py:106
  357.3 24.2 %all-to-all-done.3 = f32[32,1,12288]{2,1,0:T(1,128)} async-done(((f32[32,1,12288]{2,1,0:T(1,128)}), f32[32,1,12288]{2,1,0:T(1,128)}, u32[]{:S(2)}, u32[]{:S(2)}) %all-to-all-start.3) | async-done | bytes 1572896 | tf_op jit(solution)/shard_map/all_to_all | solution.py:46
  381.5 6.3 %reduce.3 = f32[32,12288]{1,0:T(8,128)} reduce(f32[32,1,12288]{2,1,0:T(1,128)} %all-to-all-done.3, f32[]{:T(128)} %constant.71), dimensions={1}, to_apply=%all_to_all.20.reduce_sub_computation | reduce | bytes 3145732 | tf_op jit(solution)/shard_map/all_to_all | solution.py:46
  387.8 2.8 broadcast_in_dim.128
  (67 shorter events, 27.9 us)
Async XLA Ops:
  7.2 240.5 %copy-start = (bf16[1,3,384,1024]{3,2,1,0:T(8,128)(2,1)S(1)}, bf16[1,3,384,1024]{3,2,1,0:T(8,128)(2,1)}, u32[]{:S(2)}) copy-start(bf16[1,3,384,1024]{3,2,1,0:T(8,128)(2,1)} %param.13) | copy-start | bytes 7077892
  7.2 223.8 %reduce-scatter.2.cloned.1.call-start = ((), (), s32[]{:S(2)}) async-start(), calls=%async_computation.5 | async-start | bytes 5013504 | tf_op jit(solution)/shard_map/reduce_scatter | solution.py:111
  22.7 10.2 %copy-start.4 = (bf16[128,1024]{1,0:T(8,128)(2,1)S(1)}, bf16[128,1024]{1,0:T(8,128)(2,1)}, u32[]{:S(2)}) copy-start(bf16[128,1024]{1,0:T(8,128)(2,1)} %param.7) | copy-start | bytes 786436
  157.5 2.1 copy-start.1
  163.2 2.4 copy-start.2
  163.3 2.4 copy-start.5
  173.9 64.0 %copy-start.8 = (pred[3]{0:T(512)(128)(4,1)}, pred[3]{0:T(512)(128)(4,1)S(1)}, u32[]{:S(2)}) copy-start(pred[3]{0:T(512)(128)(4,1)S(1)} %fusion.23) | copy-start | bytes 13
  174.1 63.7 %copy-start.6 = (pred[3,16]{1,0:T(4,128)(4,1)}, pred[3,16]{1,0:T(4,128)(4,1)S(1)}, u32[]{:S(2)}) copy-start(pred[3,16]{1,0:T(4,128)(4,1)S(1)} %fusion.24) | copy-start | bytes 148
  237.8 47.5 %all-to-all-start.2 = ((f32[32,1,12288]{2,1,0:T(1,128)}), f32[32,1,12288]{2,1,0:T(1,128)}, u32[]{:S(2)}, u32[]{:S(2)}) async-start(f32[32,1,12288]{2,1,0:T(1,128)} %all_to_all.21), calls=%async_computation.3 | async-start | bytes 3145728 | tf_op jit(solution)/shard_map/all_to_all | solution.py:43
  285.3 47.7 %all-to-all-start.1 = ((bf16[32,48,512]{2,1,0:T(8,128)(2,1)}), bf16[32,48,512]{2,1,0:T(8,128)(2,1)}, u32[]{:S(2)}, u32[]{:S(2)}) async-start(bf16[32,48,512]{2,1,0:T(8,128)(2,1)} %fusion.14), calls=%async_computation.1 | async-start | bytes 3145728 | tf_op jit(solution)/shard_map/all_to_all | solution.py:94
  335.6 45.9 %all-to-all-start.3 = ((f32[32,1,12288]{2,1,0:T(1,128)}), f32[32,1,12288]{2,1,0:T(1,128)}, u32[]{:S(2)}, u32[]{:S(2)}) async-start(f32[32,1,12288]{2,1,0:T(1,128)} %broadcast_in_dim.127), calls=%async_computation.4 | async-start | bytes 3145728 | tf_op jit(solution)/shard_map/all_to_all | solution.py:46
  387.8 2.8 copy-start.7
  387.8 4.8 %copy-start.3 = (f32[3,24,1024]{2,1,0:T(8,128)S(1)}, f32[3,24,1024]{2,1,0:T(8,128)}, u32[]{:S(2)}) copy-start(f32[3,24,1024]{2,1,0:T(8,128)} %reduce-scatter.2.cloned.1.call-done) | copy-start | bytes 884740
  387.8 4.8 %copy-start.9 = (pred[3]{0:T(512)(128)(4,1)S(1)}, pred[3]{0:T(512)(128)(4,1)}, u32[]{:S(2)}) copy-start(pred[3]{0:T(512)(128)(4,1)} %copy-done.8) | copy-start | bytes 13
Sparse Core Ops, SparseCore 0:
  169.4 61.5 reduce-scatter.1

commit v3 on v2

--- a/solution.py
+++ b/solution.py
@@ -30,15 +30,6 @@
     return destination * capacity + position
 
 
-def route_of_place(places, length):
-    route_count = places.shape[0]
-    return (
-        jnp.full((length,), route_count, jnp.int32)
-        .at[places]
-        .set(jnp.arange(route_count, dtype=jnp.int32))
-    )
-
-
 def exchange_sum(x, axis, count):
     pieces = lax.all_to_all(x.reshape(count, -1), axis, split_axis=0, concat_axis=0, tiled=True)
     own_total = jnp.sum(pieces, axis=0)
@@ -59,20 +50,25 @@
     route_count = tok_rows * chosen_count
     own_index = lax.axis_index("expert")
     places = buffer_places(route_expert, route_replica, flat_slots, capacity)
-    source_route = route_of_place(places, length)
-    hidden_rows = jnp.concatenate(
-        [hidden.reshape(route_count, hidden_width), jnp.zeros((1, hidden_width), hidden.dtype)],
-        axis=0,
+    lane = 128
+    spots = jnp.arange(length, dtype=jnp.int32)
+    chosen = places[None, :] == spots[:, None]
+    pick_route = chosen.astype(jnp.bfloat16)
+    pick_token = jnp.sum(
+        chosen.reshape(length, tok_rows, chosen_count).astype(jnp.int32), axis=2
+    ).astype(jnp.bfloat16)
+    route_table = jnp.concatenate(
+        [
+            hidden.reshape(route_count, hidden_width),
+            jnp.pad(gate.reshape(route_count, 1), ((0, 0), (0, lane - 1))),
+        ],
+        axis=1,
     )
-    gate_rows = jnp.concatenate([gate.reshape(route_count), jnp.zeros((1,), gate.dtype)])
-    sent_hidden = hidden_rows[source_route].reshape(groups, block_rows, hidden_width)
-    sent_gate = gate_rows[source_route].reshape(groups, block_rows)
-    padded_grad = jnp.concatenate([out_grad, jnp.zeros((1, model_width), out_grad.dtype)], axis=0)
-    token_rows = jnp.where(source_route < route_count, source_route // chosen_count, tok_rows)
-    sent_grad = padded_grad[token_rows].reshape(groups, block_rows, model_width)
-    lane = 128
-    gate_block = jnp.pad(sent_gate[..., None], ((0, 0), (0, 0), (0, lane - 1)))
-    sent = jnp.concatenate([sent_grad, sent_hidden, gate_block], axis=-1)
+    sent_grad = jnp.dot(pick_token, out_grad, preferred_element_type=jnp.float32)
+    sent_route = jnp.dot(pick_route, route_table, preferred_element_type=jnp.float32)
+    sent = jnp.concatenate(
+        [sent_grad.astype(jnp.bfloat16), sent_route.astype(jnp.bfloat16)], axis=1
+    ).reshape(groups, block_rows, model_width + hidden_width + lane)
     got = lax.all_to_all(sent, "expert", split_axis=0, concat_axis=0, tiled=True)
     got_grad = got[..., :model_width]
     got_hidden = got[..., model_width : model_width + hidden_width]

time: 401 us -> 394 us (0.983)
  local copies, waits for them, and re-layouts: 66.2 us -> 46.2 us
  other arithmetic: 24.2 us -> 32.1 us
    gather x3 -> x0, local copies, waits for them, and re-layouts: 20.6 us -> none  [the longest x1 9.46 us: per_device(): sent_gate = gate_rows[source_route].reshape(groups, block_rows)]
    reduce_sum x0 -> x1, other arithmetic: none -> 8.02 us  [per_device(): jnp.sum(chosen.reshape(length, tok_rows, chosen_count).astype(jnp.int32),...]
    concatenate x2 -> x1, local copies, waits for them, and re-layouts: 1.24 us -> 6.71 us  [per_device(): jnp.concatenate([sent_grad.astype(jnp.bfloat16), sent_route.astype(jnp.bf...]
    scatter x1 -> x0, local copies, waits for them, and re-layouts: 4.32 us -> none  [route_of_place(): return jnp.full((length,), route_count, jnp.int32).at[places].set(jnp.ara...]
    dot_general x0 -> x2, matrix products: none -> 4.02 us  [the longest x1 2.05 us: per_device(): jnp.dot(pick_token, out_grad, preferred_element_type=jnp.float32)]
where the time goes in v3:
time: 394 us; the launch traced here: 392 us
  waiting for transfers between devices  147 us (37%)
  blocking collectives  116 us (29%)
  local copies, waits for them, and re-layouts  46.2 us (12%)
  other arithmetic  32.1 us (8%)
  starting transfers between devices  24 us (6%)
  between operations  14.3 us (4%)
  matrix products  12 us (3%)
    all_to_all x1, blocking collectives, per_device(): lax.all_to_all(sent, 'expert', split_axis=0, concat_axis=0, tiled=True)  116 us
    reduce_scatter x1, waiting for transfers between devices, per_device(): lax.psum_scatter(partial_value, 'dp', scatter_dimension=1, tiled=True)  56.9 us
    all_to_all x1, waiting for transfers between devices, per_device(): lax.all_to_all(jnp.concatenate([back_rows, back_block], axis=-1), 'expert...  37.6 us
    all_to_all x1, waiting for transfers between devices, exchange_sum(): lax.all_to_all(x.reshape(count, -1), axis, split_axis=0, concat_axis=0, t...  28.9 us
    all_to_all x1, waiting for transfers between devices, exchange_sum(): lax.all_to_all(copies, axis, split_axis=0, concat_axis=0, tiled=True)  24 us
    all_to_all x1, starting transfers between devices, exchange_sum(): lax.all_to_all(x.reshape(count, -1), axis, split_axis=0, concat_axis=0, t...  9.66 us
    reduce_sum x1, other arithmetic, per_device(): jnp.sum(chosen.reshape(length, tok_rows, chosen_count).astype(jnp.int32),...  8.02 us
  transfers between devices with their start and end apart: 4, of which 4 were waited for; matrix products, arithmetic and copies ran while one was open for 8% of the time, Pallas kernels for 0%

profile of v3, /device:TPU:192, one launch (start us, length us, event | category | flops | bytes accessed | tf_op | source)
XLA Modules:
  0.0 392.4 jit_solution(12661442141593622727)
XLA Ops:
  11.0 8.0 %convert_reduce_fusion = s32[1536,128]{1,0:T(8,128)S(1)} fusion(s32[128,8]{0,1:T(8,128)S(1)} %copy.93), kind=kLoop, calls=%fused_computation.3 | loop fusion | flops 4521984 | bytes 790528 | tf_op jit(solution)/shard_map/reduce_sum | solution.py:57
  24.1 2.4 pad_maximum_fusion
  26.5 6.7 %copy.96 = bf16[1536,1536]{1,0:T(8,128)(2,1)} copy(bf16[1536,1536]{0,1:T(8,128)(2,1)} %pad_maximum_fusion) | data formatting | bytes 9437184 | tf_op jit(solution)/shard_map/concatenate | solution.py:69
  33.2 116.5 %all_to_all.26 = bf16[32,48,1536]{2,1,0:T(8,128)(2,1)S(1)} all-to-all(bf16[32,48,1536]{2,1,0:T(8,128)(2,1)} %bitcast.36), channel_id=1, replica_groups=mesh['dp'=16,'expert'=32] {'expert'}, dimensions={0} | all-to-all | bytes 9437184 | tf_op jit(solution)/shard_map/all_to_all | solution.py:72
  153.0 2.4 slice.25
  155.4 2.4 slice.26
  157.7 3.6 fusion.12
  166.2 56.9 %reduce-scatter.2.cloned.1.call-done = f32[3,24,1024]{2,1,0:T(8,128)} async-done(((f32[3,384,1024]{2,1,0:T(8,128)}), f32[3,24,1024]{2,1,0:T(8,128)}) %reduce-scatter.2.cloned.1.call-update) | async-done | bytes 294928 | tf_op jit(solution)/shard_map/reduce_scatter | solution.py:107
  223.1 2.9 select_reduce_fusion.1
  226.0 4.0 %all_to_all.21 = f32[32,1,12288]{2,1,0:T(1,128)} reshape(f32[16,24,1024]{2,1,0:T(8,128)} %select_reduce_fusion.1) | data formatting | bytes 3145728 | tf_op jit(solution)/shard_map/all_to_all | solution.py:34
  230.0 9.7 %all-to-all-start.2 = ((f32[32,1,12288]{2,1,0:T(1,128)}), f32[32,1,12288]{2,1,0:T(1,128)}, u32[]{:S(2)}, u32[]{:S(2)}) async-start(f32[32,1,12288]{2,1,0:T(1,128)} %all_to_all.21), calls=%async_computation.3 | async-start | bytes 3145728 | tf_op jit(solution)/shard_map/all_to_all | solution.py:34
  239.7 4.4 %fusion.10 = (bf16[32,3,16,384]{3,2,0,1:T(8,128)(2,1)S(1)}, bf16[32,3,16]{2,0,1:T(8,128)(2,1)}) fusion(f32[32,3,16]{2,0,1:T(8,128)} %copy.99, bf16[1,3,384,1024]{3,2,1,0:T(8,128)(2,1)S(1)} %copy-done, bf16[32,3,16,1024]{3,2,1,0:T(8,128)(2,1)} %bitcast.39, bf16[32,3,16,384]{3,2,1,0:T(8,128)(2,1)S(1)} %bitcast.41), kind=kOutput, calls=%fused_computation.24 | convolution fusion | flops 1210907136 | bytes 7873536 | tf_op jit(solution)/shard_map/xscd,sfd->xscf/dot_general | solution.py:80
  246.2 2.4 fusion.16
  248.5 28.9 %all-to-all-done.2 = f32[32,1,12288]{2,1,0:T(1,128)} async-done(((f32[32,1,12288]{2,1,0:T(1,128)}), f32[32,1,12288]{2,1,0:T(1,128)}, u32[]{:S(2)}, u32[]{:S(2)}) %all-to-all-start.2) | async-done | bytes 1572896 | tf_op jit(solution)/shard_map/all_to_all | solution.py:34
  277.4 7.7 %all-to-all-start.1 = ((bf16[32,48,512]{2,1,0:T(8,128)(2,1)}), bf16[32,48,512]{2,1,0:T(8,128)(2,1)}, u32[]{:S(2)}, u32[]{:S(2)}) async-start(bf16[32,48,512]{2,1,0:T(8,128)(2,1)} %fusion.16), calls=%async_computation.1 | async-start | bytes 3145728 | tf_op jit(solution)/shard_map/all_to_all | solution.py:90
  285.1 2.4 reduce_sum.98
  287.6 37.6 %all-to-all-done.1 = bf16[32,48,512]{2,1,0:T(8,128)(2,1)} async-done(((bf16[32,48,512]{2,1,0:T(8,128)(2,1)}), bf16[32,48,512]{2,1,0:T(8,128)(2,1)}, u32[]{:S(2)}, u32[]{:S(2)}) %all-to-all-start.1) | async-done | bytes 1572896 | tf_op jit(solution)/shard_map/all_to_all | solution.py:90
  325.2 2.6 broadcast_in_dim.112
  327.7 6.6 %all-to-all-start.3 = ((f32[32,1,12288]{2,1,0:T(1,128)}), f32[32,1,12288]{2,1,0:T(1,128)}, u32[]{:S(2)}, u32[]{:S(2)}) async-start(f32[32,1,12288]{2,1,0:T(1,128)} %broadcast_in_dim.112), calls=%async_computation.4 | async-start | bytes 3145728 | tf_op jit(solution)/shard_map/all_to_all | solution.py:37
  337.1 5.0 %gather_fusion = bf16[1024,384]{1,0:T(8,128)(2,1)} fusion(bf16[1536,384]{1,0:T(8,128)(2,1)S(1)} %bitcast.35, s32[1024]{0:T(1024)S(1)} %broadcast_clamp_fusion), kind=kCustom, calls=%fused_computation | custom fusion | bytes 1576960 | tf_op jit(solution)/shard_map/gather | solution.py:99
  342.1 6.8 %gather_fusion.1 = bf16[1024]{0:T(1024)(128)(2,1)S(1)} fusion(bf16[1536]{0:T(1024)(128)(2,1)S(1)} %reshape_squeeze.4, s32[1024]{0:T(1024)S(1)} %broadcast_clamp_fusion), kind=kCustom, calls=%fused_computation.1 | custom fusion | bytes 8192 | tf_op jit(solution)/shard_map/gather | solution.py:102
  349.7 24.0 %all-to-all-done.3 = f32[32,1,12288]{2,1,0:T(1,128)} async-done(((f32[32,1,12288]{2,1,0:T(1,128)}), f32[32,1,12288]{2,1,0:T(1,128)}, u32[]{:S(2)}, u32[]{:S(2)}) %all-to-all-start.3) | async-done | bytes 1572896 | tf_op jit(solution)/shard_map/all_to_all | solution.py:37
  373.7 6.3 %reduce.3 = f32[32,12288]{1,0:T(8,128)} reduce(f32[32,1,12288]{2,1,0:T(1,128)} %all-to-all-done.3, f32[]{:T(128)} %constant.41), dimensions={1}, to_apply=%all_to_all.20.reduce_sub_computation | reduce | bytes 3145732 | tf_op jit(solution)/shard_map/all_to_all | solution.py:37
  380.0 2.8 broadcast_in_dim.113
  (63 shorter events, 25.4 us)
Async XLA Ops:
  7.2 232.5 %copy-start = (bf16[1,3,384,1024]{3,2,1,0:T(8,128)(2,1)S(1)}, bf16[1,3,384,1024]{3,2,1,0:T(8,128)(2,1)}, u32[]{:S(2)}) copy-start(bf16[1,3,384,1024]{3,2,1,0:T(8,128)(2,1)} %param.13) | copy-start | bytes 7077892
  7.2 216.0 %reduce-scatter.2.cloned.1.call-start = ((), (), s32[]{:S(2)}) async-start(), calls=%async_computation.5 | async-start | bytes 5013504 | tf_op jit(solution)/shard_map/reduce_scatter | solution.py:107
  20.1 2.1 copy-start.9
  149.7 2.1 copy-start.1
  155.4 2.4 copy-start.2
  155.4 2.4 copy-start.4
  166.0 64.0 %copy-start.7 = (pred[3]{0:T(512)(128)(4,1)}, pred[3]{0:T(512)(128)(4,1)S(1)}, u32[]{:S(2)}) copy-start(pred[3]{0:T(512)(128)(4,1)S(1)} %fusion.27) | copy-start | bytes 13
  166.2 63.7 %copy-start.5 = (pred[3,16]{1,0:T(4,128)(4,1)}, pred[3,16]{1,0:T(4,128)(4,1)S(1)}, u32[]{:S(2)}) copy-start(pred[3,16]{1,0:T(4,128)(4,1)S(1)} %fusion.28) | copy-start | bytes 148
  230.0 47.5 %all-to-all-start.2 = ((f32[32,1,12288]{2,1,0:T(1,128)}), f32[32,1,12288]{2,1,0:T(1,128)}, u32[]{:S(2)}, u32[]{:S(2)}) async-start(f32[32,1,12288]{2,1,0:T(1,128)} %all_to_all.21), calls=%async_computation.3 | async-start | bytes 3145728 | tf_op jit(solution)/shard_map/all_to_all | solution.py:34
  277.4 47.7 %all-to-all-start.1 = ((bf16[32,48,512]{2,1,0:T(8,128)(2,1)}), bf16[32,48,512]{2,1,0:T(8,128)(2,1)}, u32[]{:S(2)}, u32[]{:S(2)}) async-start(bf16[32,48,512]{2,1,0:T(8,128)(2,1)} %fusion.16), calls=%async_computation.1 | async-start | bytes 3145728 | tf_op jit(solution)/shard_map/all_to_all | solution.py:90
  327.7 45.9 %all-to-all-start.3 = ((f32[32,1,12288]{2,1,0:T(1,128)}), f32[32,1,12288]{2,1,0:T(1,128)}, u32[]{:S(2)}, u32[]{:S(2)}) async-start(f32[32,1,12288]{2,1,0:T(1,128)} %broadcast_in_dim.112), calls=%async_computation.4 | async-start | bytes 3145728 | tf_op jit(solution)/shard_map/all_to_all | solution.py:37
  380.0 2.8 copy-start.6
  380.0 4.8 %copy-start.3 = (f32[3,24,1024]{2,1,0:T(8,128)S(1)}, f32[3,24,1024]{2,1,0:T(8,128)}, u32[]{:S(2)}) copy-start(f32[3,24,1024]{2,1,0:T(8,128)} %reduce-scatter.2.cloned.1.call-done) | copy-start | bytes 884740
  380.0 4.8 %copy-start.8 = (pred[3]{0:T(512)(128)(4,1)S(1)}, pred[3]{0:T(512)(128)(4,1)}, u32[]{:S(2)}) copy-start(pred[3]{0:T(512)(128)(4,1)} %copy-done.7) | copy-start | bytes 13
Sparse Core Ops, SparseCore 0:
  161.5 61.5 reduce-scatter.1

commit v4 on v3

--- a/solution.py
+++ b/solution.py
@@ -54,9 +54,13 @@
     spots = jnp.arange(length, dtype=jnp.int32)
     chosen = places[None, :] == spots[:, None]
     pick_route = chosen.astype(jnp.bfloat16)
-    pick_token = jnp.sum(
-        chosen.reshape(length, tok_rows, chosen_count).astype(jnp.int32), axis=2
+    route_token = (
+        jnp.arange(route_count, dtype=jnp.int32)[:, None] // chosen_count
+        == jnp.arange(tok_rows, dtype=jnp.int32)[None, :]
     ).astype(jnp.bfloat16)
+    pick_token = jnp.dot(pick_route, route_token, preferred_element_type=jnp.float32).astype(
+        jnp.bfloat16
+    )
     route_table = jnp.concatenate(
         [
             hidden.reshape(route_count, hidden_width),
@@ -64,11 +68,19 @@
         ],
         axis=1,
     )
-    sent_grad = jnp.dot(pick_token, out_grad, preferred_element_type=jnp.float32)
-    sent_route = jnp.dot(pick_route, route_table, preferred_element_type=jnp.float32)
-    sent = jnp.concatenate(
-        [sent_grad.astype(jnp.bfloat16), sent_route.astype(jnp.bfloat16)], axis=1
-    ).reshape(groups, block_rows, model_width + hidden_width + lane)
+    block_table = jnp.concatenate(
+        [
+            jnp.pad(out_grad, ((0, 0), (0, hidden_width + lane))),
+            jnp.pad(route_table, ((0, 0), (model_width, 0))),
+        ],
+        axis=0,
+    )
+    picks = jnp.concatenate([pick_token, pick_route], axis=1)
+    sent = (
+        jnp.dot(picks, block_table, preferred_element_type=jnp.float32)
+        .astype(jnp.bfloat16)
+        .reshape(groups, block_rows, model_width + hidden_width + lane)
+    )
     got = lax.all_to_all(sent, "expert", split_axis=0, concat_axis=0, tiled=True)
     got_grad = got[..., :model_width]
     got_hidden = got[..., model_width : model_width + hidden_width]

time: 394 us -> 387 us (0.982)
  other arithmetic: 32.1 us -> 24.9 us
  matrix products: 12 us -> 18.9 us
  local copies, waits for them, and re-layouts: 46.2 us -> 40.6 us
    reduce_sum x1 -> x0, other arithmetic: 8.02 us -> none  [per_device(): jnp.sum(chosen.reshape(length, tok_rows, chosen_count).astype(jnp.int32),...]
    dot_general x2, matrix products: 4.02 us -> 10.9 us  [the longest x1 8.62 us: per_device(): jnp.dot(picks, block_table, preferred_element_type=jnp.float32)]
    concatenate x1 -> x0, local copies, waits for them, and re-layouts: 6.71 us -> none  [per_device(): jnp.concatenate([sent_grad.astype(jnp.bfloat16), sent_route.astype(jnp.bf...]
where the time goes in v4:
time: 387 us; the launch traced here: 386 us
  waiting for transfers between devices  147 us (38%)
  blocking collectives  116 us (30%)
  local copies, waits for them, and re-layouts  40.6 us (10%)
  other arithmetic  24.9 us (6%)
  starting transfers between devices  23.9 us (6%)
  matrix products  18.9 us (5%)
  between operations  14.3 us (4%)
    all_to_all x1, blocking collectives, per_device(): lax.all_to_all(sent, 'expert', split_axis=0, concat_axis=0, tiled=True)  116 us
    reduce_scatter x1, waiting for transfers between devices, per_device(): lax.psum_scatter(partial_value, 'dp', scatter_dimension=1, tiled=True)  56.9 us
    all_to_all x1, waiting for transfers between devices, per_device(): lax.all_to_all(jnp.concatenate([back_rows, back_block], axis=-1), 'expert...  37.6 us
    all_to_all x1, waiting for transfers between devices, exchange_sum(): lax.all_to_all(x.reshape(count, -1), axis, split_axis=0, concat_axis=0, t...  28.9 us
    all_to_all x1, waiting for transfers between devices, exchange_sum(): lax.all_to_all(copies, axis, split_axis=0, concat_axis=0, tiled=True)  24 us
    all_to_all x1, starting transfers between devices, exchange_sum(): lax.all_to_all(x.reshape(count, -1), axis, split_axis=0, concat_axis=0, t...  9.6 us
    dot_general x1, matrix products, per_device(): jnp.dot(picks, block_table, preferred_element_type=jnp.float32)  8.62 us
  transfers between devices with their start and end apart: 4, of which 4 were waited for; matrix products, arithmetic and copies ran while one was open for 8% of the time, Pallas kernels for 0%

profile of v4, /device:TPU:192, one launch (start us, length us, event | category | flops | bytes accessed | tf_op | source)
XLA Modules:
  0.0 386.3 jit_solution(3808556667372697557)
XLA Ops:
  10.9 3.2 fusion.2
  14.1 2.3 fusion.20
  18.7 8.6 %convolution_convert_fusion = bf16[1536,1536]{1,0:T(8,128)(2,1)S(1)} fusion(bf16[1024,512]{1,0:T(8,128)(2,1)S(1)} %fusion.31, bf16[128,1024]{1,0:T(8,128)(2,1)} %param.7, bf16[1536,1024]{1,0:T(8,128)(2,1)} %fusion.2, bf16[1536,128]{1,0:T(8,128)(2,1)} %copy.71), kind=kOutput, calls=%fused_computation.2 | convolution fusion | flops 5459410944 | bytes 9568256 | tf_op jit(solution)/shard_map/dot_general | solution.py:80
  27.3 116.3 %all_to_all.26 = bf16[32,48,1536]{2,1,0:T(8,128)(2,1)S(1)} all-to-all(bf16[32,48,1536]{2,1,0:T(8,128)(2,1)S(1)} %bitcast.37), channel_id=1, replica_groups=mesh['dp'=16,'expert'=32] {'expert'}, dimensions={0} | all-to-all | bytes 9437184 | tf_op jit(solution)/shard_map/all_to_all | solution.py:84
  146.9 2.4 slice.25
  149.3 2.3 slice.26
  151.6 3.6 fusion.24
  160.1 56.9 %reduce-scatter.2.cloned.1.call-done = f32[3,24,1024]{2,1,0:T(8,128)} async-done(((f32[3,384,1024]{2,1,0:T(8,128)}), f32[3,24,1024]{2,1,0:T(8,128)}) %reduce-scatter.2.cloned.1.call-update) | async-done | bytes 294928 | tf_op jit(solution)/shard_map/reduce_scatter | solution.py:119
  217.1 2.9 select_reduce_fusion.1
  219.9 4.0 %all_to_all.21 = f32[32,1,12288]{2,1,0:T(1,128)} reshape(f32[16,24,1024]{2,1,0:T(8,128)} %select_reduce_fusion.1) | data formatting | bytes 3145728 | tf_op jit(solution)/shard_map/all_to_all | solution.py:34
  223.9 9.6 %all-to-all-start.2 = ((f32[32,1,12288]{2,1,0:T(1,128)}), f32[32,1,12288]{2,1,0:T(1,128)}, u32[]{:S(2)}, u32[]{:S(2)}) async-start(f32[32,1,12288]{2,1,0:T(1,128)} %all_to_all.21), calls=%async_computation.3 | async-start | bytes 3145728 | tf_op jit(solution)/shard_map/all_to_all | solution.py:34
  233.5 4.4 %fusion.22 = (bf16[32,3,16,384]{3,2,0,1:T(8,128)(2,1)S(1)}, bf16[32,3,16]{2,0,1:T(8,128)(2,1)}) fusion(f32[32,3,16]{2,0,1:T(8,128)} %copy.75, bf16[1,3,384,1024]{3,2,1,0:T(8,128)(2,1)S(1)} %copy-done, bf16[32,3,16,1024]{3,2,1,0:T(8,128)(2,1)} %bitcast.39, bf16[32,3,16,384]{3,2,1,0:T(8,128)(2,1)S(1)} %bitcast.41), kind=kOutput, calls=%fused_computation.33 | convolution fusion | flops 1210907136 | bytes 7873536 | tf_op jit(solution)/shard_map/xscd,sfd->xscf/dot_general | solution.py:92
  240.0 2.4 fusion.29
  242.4 28.9 %all-to-all-done.2 = f32[32,1,12288]{2,1,0:T(1,128)} async-done(((f32[32,1,12288]{2,1,0:T(1,128)}), f32[32,1,12288]{2,1,0:T(1,128)}, u32[]{:S(2)}, u32[]{:S(2)}) %all-to-all-start.2) | async-done | bytes 1572896 | tf_op jit(solution)/shard_map/all_to_all | solution.py:34
  271.3 7.7 %all-to-all-start.1 = ((bf16[32,48,512]{2,1,0:T(8,128)(2,1)}), bf16[32,48,512]{2,1,0:T(8,128)(2,1)}, u32[]{:S(2)}, u32[]{:S(2)}) async-start(bf16[32,48,512]{2,1,0:T(8,128)(2,1)} %fusion.29), calls=%async_computation.1 | async-start | bytes 3145728 | tf_op jit(solution)/shard_map/all_to_all | solution.py:102
  279.0 2.4 reduce_sum.88
  281.5 37.6 %all-to-all-done.1 = bf16[32,48,512]{2,1,0:T(8,128)(2,1)} async-done(((bf16[32,48,512]{2,1,0:T(8,128)(2,1)}), bf16[32,48,512]{2,1,0:T(8,128)(2,1)}, u32[]{:S(2)}, u32[]{:S(2)}) %all-to-all-start.1) | async-done | bytes 1572896 | tf_op jit(solution)/shard_map/all_to_all | solution.py:102
  319.1 2.6 broadcast_in_dim.114
  321.6 6.6 %all-to-all-start.3 = ((f32[32,1,12288]{2,1,0:T(1,128)}), f32[32,1,12288]{2,1,0:T(1,128)}, u32[]{:S(2)}, u32[]{:S(2)}) async-start(f32[32,1,12288]{2,1,0:T(1,128)} %broadcast_in_dim.114), calls=%async_computation.4 | async-start | bytes 3145728 | tf_op jit(solution)/shard_map/all_to_all | solution.py:37
  331.0 5.0 %gather_fusion = bf16[1024,384]{1,0:T(8,128)(2,1)} fusion(bf16[1536,384]{1,0:T(8,128)(2,1)S(1)} %bitcast.35, s32[1024]{0:T(1024)S(1)} %broadcast_clamp_fusion), kind=kCustom, calls=%fused_computation | custom fusion | bytes 1576960 | tf_op jit(solution)/shard_map/gather | solution.py:111
  336.0 6.8 %gather_fusion.1 = bf16[1024]{0:T(1024)(128)(2,1)S(1)} fusion(bf16[1536]{0:T(1024)(128)(2,1)S(1)} %reshape_squeeze.4, s32[1024]{0:T(1024)S(1)} %broadcast_clamp_fusion), kind=kCustom, calls=%fused_computation.1 | custom fusion | bytes 8192 | tf_op jit(solution)/shard_map/gather | solution.py:114
  343.6 24.0 %all-to-all-done.3 = f32[32,1,12288]{2,1,0:T(1,128)} async-done(((f32[32,1,12288]{2,1,0:T(1,128)}), f32[32,1,12288]{2,1,0:T(1,128)}, u32[]{:S(2)}, u32[]{:S(2)}) %all-to-all-start.3) | async-done | bytes 1572896 | tf_op jit(solution)/shard_map/all_to_all | solution.py:37
  367.5 6.3 %reduce.3 = f32[32,12288]{1,0:T(8,128)} reduce(f32[32,1,12288]{2,1,0:T(1,128)} %all-to-all-done.3, f32[]{:T(128)} %constant.60), dimensions={1}, to_apply=%all_to_all.20.reduce_sub_computation | reduce | bytes 3145732 | tf_op jit(solution)/shard_map/all_to_all | solution.py:37
  373.9 2.8 broadcast_in_dim.115
  (62 shorter events, 22.6 us)
Async XLA Ops:
  7.2 226.4 %copy-start = (bf16[1,3,384,1024]{3,2,1,0:T(8,128)(2,1)S(1)}, bf16[1,3,384,1024]{3,2,1,0:T(8,128)(2,1)}, u32[]{:S(2)}) copy-start(bf16[1,3,384,1024]{3,2,1,0:T(8,128)(2,1)} %param.13) | copy-start | bytes 7077892
  7.2 209.9 %reduce-scatter.2.cloned.1.call-start = ((), (), s32[]{:S(2)}) async-start(), calls=%async_computation.5 | async-start | bytes 5013504 | tf_op jit(solution)/shard_map/reduce_scatter | solution.py:119
  10.9 7.4 %copy-start.6 = (bf16[128,8]{0,1:T(8,128)(2,1)S(1)}, bf16[128,8]{0,1:T(8,128)(2,1)}, u32[]{:S(2)}) copy-start(bf16[128,8]{0,1:T(8,128)(2,1)} %param.9) | copy-start | bytes 6148
  10.9 7.7 %copy-start.4 = (bf16[128,8,384]{2,1,0:T(8,128)(2,1)S(1)}, bf16[128,8,384]{2,1,0:T(8,128)(2,1)}, u32[]{:S(2)}) copy-start(bf16[128,8,384]{2,1,0:T(8,128)(2,1)} %param.8) | copy-start | bytes 2359300
  143.6 2.1 copy-start.1
  146.9 4.7 %copy-start.5 = (f32[32,3,16]{2,0,1:T(8,128)S(1)}, f32[32,3,16]{2,0,1:T(8,128)}, u32[]{:S(2)}) copy-start(f32[32,3,16]{2,0,1:T(8,128)} %copy.75) | copy-start | bytes 18436
  149.3 2.3 copy-start.2
  159.9 64.0 %copy-start.9 = (pred[3]{0:T(512)(128)(4,1)}, pred[3]{0:T(512)(128)(4,1)S(1)}, u32[]{:S(2)}) copy-start(pred[3]{0:T(512)(128)(4,1)S(1)} %fusion.38) | copy-start | bytes 13
  160.1 63.8 %copy-start.7 = (pred[3,16]{1,0:T(4,128)(4,1)}, pred[3,16]{1,0:T(4,128)(4,1)S(1)}, u32[]{:S(2)}) copy-start(pred[3,16]{1,0:T(4,128)(4,1)S(1)} %fusion.39) | copy-start | bytes 148
  223.9 47.4 %all-to-all-start.2 = ((f32[32,1,12288]{2,1,0:T(1,128)}), f32[32,1,12288]{2,1,0:T(1,128)}, u32[]{:S(2)}, u32[]{:S(2)}) async-start(f32[32,1,12288]{2,1,0:T(1,128)} %all_to_all.21), calls=%async_computation.3 | async-start | bytes 3145728 | tf_op jit(solution)/shard_map/all_to_all | solution.py:34
  271.3 47.7 %all-to-all-start.1 = ((bf16[32,48,512]{2,1,0:T(8,128)(2,1)}), bf16[32,48,512]{2,1,0:T(8,128)(2,1)}, u32[]{:S(2)}, u32[]{:S(2)}) async-start(bf16[32,48,512]{2,1,0:T(8,128)(2,1)} %fusion.29), calls=%async_computation.1 | async-start | bytes 3145728 | tf_op jit(solution)/shard_map/all_to_all | solution.py:102
  321.6 45.9 %all-to-all-start.3 = ((f32[32,1,12288]{2,1,0:T(1,128)}), f32[32,1,12288]{2,1,0:T(1,128)}, u32[]{:S(2)}, u32[]{:S(2)}) async-start(f32[32,1,12288]{2,1,0:T(1,128)} %broadcast_in_dim.114), calls=%async_computation.4 | async-start | bytes 3145728 | tf_op jit(solution)/shard_map/all_to_all | solution.py:37
  343.6 33.1 %copy-start.8 = (pred[3,16]{1,0:T(4,128)(4,1)S(1)}, pred[3,16]{1,0:T(4,128)(4,1)}, u32[]{:S(2)}) copy-start(pred[3,16]{1,0:T(4,128)(4,1)} %copy-done.7) | copy-start | bytes 148
  373.9 4.8 %copy-start.3 = (f32[3,24,1024]{2,1,0:T(8,128)S(1)}, f32[3,24,1024]{2,1,0:T(8,128)}, u32[]{:S(2)}) copy-start(f32[3,24,1024]{2,1,0:T(8,128)} %reduce-scatter.2.cloned.1.call-done) | copy-start | bytes 884740
  373.9 4.8 %copy-start.10 = (pred[3]{0:T(512)(128)(4,1)S(1)}, pred[3]{0:T(512)(128)(4,1)}, u32[]{:S(2)}) copy-start(pred[3]{0:T(512)(128)(4,1)} %copy-done.9) | copy-start | bytes 13
Sparse Core Ops, SparseCore 0:
  155.4 61.6 reduce-scatter.1

commit v5 on v4

--- a/solution.py
+++ b/solution.py
@@ -31,8 +31,10 @@
 
 
 def exchange_sum(x, axis, count):
-    pieces = lax.all_to_all(x.reshape(count, -1), axis, split_axis=0, concat_axis=0, tiled=True)
-    own_total = jnp.sum(pieces, axis=0)
+    pieces = lax.all_to_all(
+        x.reshape(count, 8, -1).astype(jnp.bfloat16), axis, split_axis=0, concat_axis=0, tiled=True
+    )
+    own_total = jnp.sum(pieces.astype(jnp.float32), axis=0)
     copies = jnp.broadcast_to(own_total[None], pieces.shape)
     totals = lax.all_to_all(copies, axis, split_axis=0, concat_axis=0, tiled=True)
     return totals.reshape(x.shape)
@@ -128,7 +130,7 @@
     member = (slot_rank[:, None] == jnp.arange(HOT, dtype=jnp.int32)[None, :]) & slot_hot[:, None]
     hot_table = jnp.sum(jnp.where(member[:, :, None, None], group_sum[:, None], 0.0), axis=0)
     hot_total = exchange_sum(hot_table, "expert", lax.axis_size("expert"))
-    from_table = jnp.sum(jnp.where(member[:, :, None, None], hot_total[None], 0.0), axis=1)
+    from_table = hot_total[jnp.clip(slot_rank, 0, HOT - 1)]
     d_weight = jnp.where(slot_hot[:, None, None], from_table, group_sum)[None]
     return (d_hidden, d_gate, d_weight)
 

time: 387 us -> 360 us (0.930)
  other arithmetic: 24.9 us -> 11.5 us
  waiting for transfers between devices: 147 us -> 134 us
    all_to_all x1, waiting for transfers between devices: 28.9 us -> 10.5 us  [exchange_sum(): lax.all_to_all(x.reshape(count, 8, -1).astype(jnp.bfloat16), axis, split_...]
    all_to_all x1 -> x0, other arithmetic: 6.31 us -> none  [exchange_sum(): lax.all_to_all(copies, axis, split_axis=0, concat_axis=0, tiled=True)]
    all_to_all x1 -> x0, local copies, waits for them, and re-layouts: 3.98 us -> none  [exchange_sum(): lax.all_to_all(x.reshape(count, -1), axis, split_axis=0, concat_axis=0, t...]
where the time goes in v5:
time: 360 us; the launch traced here: 359 us
  waiting for transfers between devices  134 us (37%)
  blocking collectives  116 us (32%)
  local copies, waits for them, and re-layouts  38.6 us (11%)
  starting transfers between devices  24.7 us (7%)
  matrix products  19.2 us (5%)
  between operations  14.3 us (4%)
  other arithmetic  11.5 us (3%)
    all_to_all x1, blocking collectives, per_device(): lax.all_to_all(sent, 'expert', split_axis=0, concat_axis=0, tiled=True)  116 us
    reduce_scatter x1, waiting for transfers between devices, per_device(): lax.psum_scatter(partial_value, 'dp', scatter_dimension=1, tiled=True)  60.8 us
    all_to_all x1, waiting for transfers between devices, per_device(): lax.all_to_all(jnp.concatenate([back_rows, back_block], axis=-1), 'expert...  39.1 us
    all_to_all x1, waiting for transfers between devices, exchange_sum(): lax.all_to_all(copies, axis, split_axis=0, concat_axis=0, tiled=True)  23.6 us
    all_to_all x1, waiting for transfers between devices, exchange_sum(): lax.all_to_all(x.reshape(count, 8, -1).astype(jnp.bfloat16), axis, split_...  10.5 us
    all_to_all x1, starting transfers between devices, exchange_sum(): lax.all_to_all(x.reshape(count, 8, -1).astype(jnp.bfloat16), axis, split_...  9.78 us
    dot_general x1, matrix products, per_device(): jnp.dot(picks, block_table, preferred_element_type=jnp.float32)  8.62 us
    all_to_all x1, starting transfers between devices, per_device(): lax.all_to_all(jnp.concatenate([back_rows, back_block], axis=-1), 'expert...  8.42 us
  transfers between devices with their start and end apart: 4, of which 4 were waited for; matrix products, arithmetic and copies ran while one was open for 8% of the time, Pallas kernels for 0%

profile of v5, /device:TPU:192, one launch (start us, length us, event | category | flops | bytes accessed | tf_op | source)
XLA Modules:
  0.0 358.7 jit_solution(7980141678033157336)
XLA Ops:
  10.9 3.2 fusion.2
  14.1 2.3 fusion.20
  16.3 1.9 copy.70
  18.7 8.6 %convolution_convert_fusion = bf16[1536,1536]{1,0:T(8,128)(2,1)S(1)} fusion(bf16[1024,512]{1,0:T(8,128)(2,1)S(1)} %fusion.31, bf16[128,1024]{1,0:T(8,128)(2,1)} %param.7, bf16[1536,1024]{1,0:T(8,128)(2,1)} %fusion.2, bf16[1536,128]{1,0:T(8,128)(2,1)} %copy.70), kind=kOutput, calls=%fused_computation.3 | convolution fusion | flops 5459410944 | bytes 9568256 | tf_op jit(solution)/shard_map/dot_general | solution.py:82
  27.3 116.3 %all_to_all.20 = bf16[32,48,1536]{2,1,0:T(8,128)(2,1)S(1)} all-to-all(bf16[32,48,1536]{2,1,0:T(8,128)(2,1)S(1)} %bitcast.41), channel_id=1, replica_groups=mesh['dp'=16,'expert'=32] {'expert'}, dimensions={0} | all-to-all | bytes 9437184 | tf_op jit(solution)/shard_map/all_to_all | solution.py:86
  143.6 2.1 copy-done.1
  146.3 2.4 slice.27
  148.7 2.3 slice.28
  152.1 3.6 %fusion.24 = f32[3,384,1024]{2,1,0:T(8,128)} fusion(bf16[32,3,16,1024]{3,2,1,0:T(8,128)(2,1)S(1)} %bitcast.42, f32[32,3,16]{2,0,1:T(8,128)S(1)} %copy.74, bf16[32,3,16,384]{3,2,1,0:T(8,128)(2,1)S(1)} %bitcast.44), kind=kOutput, calls=%fused_computation.36 | convolution fusion | flops 1209729024 | bytes 9050112 | tf_op jit(solution)/shard_map/xscf,xscd->sfd/dot_general | solution.py:118
  156.7 60.8 %reduce-scatter.2.cloned.1.call-done = f32[3,24,1024]{2,1,0:T(8,128)} async-done(((f32[3,384,1024]{2,1,0:T(8,128)}), f32[3,24,1024]{2,1,0:T(8,128)}) %reduce-scatter.2.cloned.1.call-update) | async-done | bytes 294928 | tf_op jit(solution)/shard_map/reduce_scatter | solution.py:121
  217.6 1.5 select_reduce_fusion
  220.4 9.8 %all-to-all-start.2 = ((bf16[32,8,1536]{2,1,0:T(8,128)(2,1)}), bf16[32,8,1536]{2,1,0:T(8,128)(2,1)}, u32[]{:S(2)}, u32[]{:S(2)}) async-start(bf16[32,8,1536]{2,1,0:T(8,128)(2,1)} %convert_element_type.104), calls=%async_computation.3 | async-start | bytes 1572864 | tf_op jit(solution)/shard_map/all_to_all | solution.py:34
  230.2 4.7 %fusion.22 = (bf16[32,3,16,384]{3,2,0,1:T(8,128)(2,1)S(1)}, bf16[32,3,16]{2,0,1:T(8,128)(2,1)}) fusion(f32[32,3,16]{2,0,1:T(8,128)S(1)} %copy.74, bf16[1,3,384,1024]{3,2,1,0:T(8,128)(2,1)S(1)} %copy-done, bf16[32,3,16,1024]{3,2,1,0:T(8,128)(2,1)} %bitcast.43, bf16[32,3,16,384]{3,2,1,0:T(8,128)(2,1)} %bitcast.45), kind=kOutput, calls=%fused_computation.33 | convolution fusion | flops 1210907136 | bytes 7873536 | tf_op jit(solution)/shard_map/xscd,sfd->xscf/dot_general | solution.py:94
  237.1 2.4 fusion.29
  239.5 10.5 %all-to-all-done.2 = bf16[32,8,1536]{2,1,0:T(8,128)(2,1)} async-done(((bf16[32,8,1536]{2,1,0:T(8,128)(2,1)}), bf16[32,8,1536]{2,1,0:T(8,128)(2,1)}, u32[]{:S(2)}, u32[]{:S(2)}) %all-to-all-start.2) | async-done | bytes 786464 | tf_op jit(solution)/shard_map/all_to_all | solution.py:34
  250.0 8.4 %all-to-all-start.1 = ((bf16[32,48,512]{2,1,0:T(8,128)(2,1)}), bf16[32,48,512]{2,1,0:T(8,128)(2,1)}, u32[]{:S(2)}, u32[]{:S(2)}) async-start(bf16[32,48,512]{2,1,0:T(8,128)(2,1)} %fusion.29), calls=%async_computation.1 | async-start | bytes 3145728 | tf_op jit(solution)/shard_map/all_to_all | solution.py:104
  259.7 39.1 %all-to-all-done.1 = bf16[32,48,512]{2,1,0:T(8,128)(2,1)} async-done(((bf16[32,48,512]{2,1,0:T(8,128)(2,1)}), bf16[32,48,512]{2,1,0:T(8,128)(2,1)}, u32[]{:S(2)}, u32[]{:S(2)}) %all-to-all-start.1) | async-done | bytes 1572896 | tf_op jit(solution)/shard_map/all_to_all | solution.py:104
  300.1 6.5 %all-to-all-start.3 = ((f32[32,8,1536]{2,1,0:T(8,128)}), f32[32,8,1536]{2,1,0:T(8,128)}, u32[]{:S(2)}, u32[]{:S(2)}) async-start(f32[32,8,1536]{2,1,0:T(8,128)} %broadcast_in_dim.61), calls=%async_computation.4 | async-start | bytes 3145728 | tf_op jit(solution)/shard_map/all_to_all | solution.py:39
  308.6 1.4 slice.29
  310.0 5.0 %gather_fusion = bf16[1024,384]{1,0:T(8,128)(2,1)} fusion(bf16[1536,384]{1,0:T(8,128)(2,1)S(1)} %bitcast.39, s32[1024]{0:T(1024)S(1)} %broadcast_clamp_fusion), kind=kCustom, calls=%fused_computation | custom fusion | bytes 1576960 | tf_op jit(solution)/shard_map/gather | solution.py:113
  315.0 6.8 %gather_fusion.1 = bf16[1024]{0:T(1024)(128)(2,1)S(1)} fusion(bf16[1536]{0:T(1024)(128)(2,1)S(1)} %reshape_squeeze.4, s32[1024]{0:T(1024)S(1)} %broadcast_clamp_fusion), kind=kCustom, calls=%fused_computation.1 | custom fusion | bytes 8192 | tf_op jit(solution)/shard_map/gather | solution.py:116
  322.5 23.6 %all-to-all-done.3 = f32[32,8,1536]{2,1,0:T(8,128)} async-done(((f32[32,8,1536]{2,1,0:T(8,128)}), f32[32,8,1536]{2,1,0:T(8,128)}, u32[]{:S(2)}, u32[]{:S(2)}) %all-to-all-start.3) | async-done | bytes 1572896 | tf_op jit(solution)/shard_map/all_to_all | solution.py:39
  346.2 2.7 reshape.241
  348.9 2.1 gather_fusion.2
  (63 shorter events, 16.4 us)
Async XLA Ops:
  7.2 223.1 %copy-start = (bf16[1,3,384,1024]{3,2,1,0:T(8,128)(2,1)S(1)}, bf16[1,3,384,1024]{3,2,1,0:T(8,128)(2,1)}, u32[]{:S(2)}) copy-start(bf16[1,3,384,1024]{3,2,1,0:T(8,128)(2,1)} %param.13) | copy-start | bytes 7077892
  7.2 210.4 %reduce-scatter.2.cloned.1.call-start = ((), (), s32[]{:S(2)}) async-start(), calls=%async_computation.5 | async-start | bytes 5013504 | tf_op jit(solution)/shard_map/reduce_scatter | solution.py:121
  10.9 7.4 %copy-start.6 = (bf16[128,8]{0,1:T(8,128)(2,1)S(1)}, bf16[128,8]{0,1:T(8,128)(2,1)}, u32[]{:S(2)}) copy-start(bf16[128,8]{0,1:T(8,128)(2,1)} %param.9) | copy-start | bytes 6148
  10.9 7.7 %copy-start.5 = (bf16[128,8,384]{2,1,0:T(8,128)(2,1)S(1)}, bf16[128,8,384]{2,1,0:T(8,128)(2,1)}, u32[]{:S(2)}) copy-start(bf16[128,8,384]{2,1,0:T(8,128)(2,1)} %param.8) | copy-start | bytes 2359300
  143.6 2.1 copy-start.1
  148.7 2.3 copy-start.2
  151.0 1.1 copy-start.3
  156.5 78.5 %copy-start.9 = (s32[3]{0:T(128)}, s32[3]{0:T(128)S(1)}, u32[]{:S(2)}) copy-start(s32[3]{0:T(128)S(1)} %select_reduce_fusion.2) | copy-start | bytes 40
  156.7 78.3 %copy-start.7 = (pred[3]{0:T(512)(128)(4,1)}, pred[3]{0:T(512)(128)(4,1)S(1)}, u32[]{:S(2)}) copy-start(pred[3]{0:T(512)(128)(4,1)S(1)} %fusion.38) | copy-start | bytes 13
  220.4 29.6 %all-to-all-start.2 = ((bf16[32,8,1536]{2,1,0:T(8,128)(2,1)}), bf16[32,8,1536]{2,1,0:T(8,128)(2,1)}, u32[]{:S(2)}, u32[]{:S(2)}) async-start(bf16[32,8,1536]{2,1,0:T(8,128)(2,1)} %convert_element_type.104), calls=%async_computation.3 | async-start | bytes 1572864 | tf_op jit(solution)/shard_map/all_to_all | solution.py:34
  250.0 48.8 %all-to-all-start.1 = ((bf16[32,48,512]{2,1,0:T(8,128)(2,1)}), bf16[32,48,512]{2,1,0:T(8,128)(2,1)}, u32[]{:S(2)}, u32[]{:S(2)}) async-start(bf16[32,48,512]{2,1,0:T(8,128)(2,1)} %fusion.29), calls=%async_computation.1 | async-start | bytes 3145728 | tf_op jit(solution)/shard_map/all_to_all | solution.py:104
  258.4 48.1 %copy-start.10 = (s32[3]{0:T(128)S(1)}, s32[3]{0:T(128)}, u32[]{:S(2)}) copy-start(s32[3]{0:T(128)} %copy-done.9) | copy-start | bytes 40
  300.1 46.1 %all-to-all-start.3 = ((f32[32,8,1536]{2,1,0:T(8,128)}), f32[32,8,1536]{2,1,0:T(8,128)}, u32[]{:S(2)}, u32[]{:S(2)}) async-start(f32[32,8,1536]{2,1,0:T(8,128)} %broadcast_in_dim.61), calls=%async_computation.4 | async-start | bytes 3145728 | tf_op jit(solution)/shard_map/all_to_all | solution.py:39
  315.0 36.0 %copy-start.4 = (f32[3,24,1024]{2,1,0:T(8,128)S(1)}, f32[3,24,1024]{2,1,0:T(8,128)}, u32[]{:S(2)}) copy-start(f32[3,24,1024]{2,1,0:T(8,128)} %reduce-scatter.2.cloned.1.call-done) | copy-start | bytes 884740
  315.0 36.0 %copy-start.8 = (pred[3]{0:T(512)(128)(4,1)S(1)}, pred[3]{0:T(512)(128)(4,1)}, u32[]{:S(2)}) copy-start(pred[3]{0:T(512)(128)(4,1)} %copy-done.7) | copy-start | bytes 13
Sparse Core Ops, SparseCore 0:
  155.9 61.6 reduce-scatter.1

commit v6 on v5

--- a/solution.py
+++ b/solution.py
@@ -32,9 +32,9 @@
 
 def exchange_sum(x, axis, count):
     pieces = lax.all_to_all(
-        x.reshape(count, 8, -1).astype(jnp.bfloat16), axis, split_axis=0, concat_axis=0, tiled=True
+        x.reshape(count, 8, -1), axis, split_axis=0, concat_axis=0, tiled=True
     )
-    own_total = jnp.sum(pieces.astype(jnp.float32), axis=0)
+    own_total = jnp.sum(pieces, axis=0)
     copies = jnp.broadcast_to(own_total[None], pieces.shape)
     totals = lax.all_to_all(copies, axis, split_axis=0, concat_axis=0, tiled=True)
     return totals.reshape(x.shape)
@@ -128,9 +128,17 @@
     slot_hot = jnp.any(picks & is_hot[None, :], axis=1)
     slot_rank = jnp.sum(jnp.where(picks, hot_rank[None, :], 0), axis=1)
     member = (slot_rank[:, None] == jnp.arange(HOT, dtype=jnp.int32)[None, :]) & slot_hot[:, None]
-    hot_table = jnp.sum(jnp.where(member[:, :, None, None], group_sum[:, None], 0.0), axis=0)
-    hot_total = exchange_sum(hot_table, "expert", lax.axis_size("expert"))
-    from_table = hot_total[jnp.clip(slot_rank, 0, HOT - 1)]
+    expert_count = lax.axis_size("expert")
+    halves = expert_count // HOT
+    chunk_rows = 8
+    chunked = group_sum.reshape(slots, halves, chunk_rows, -1)
+    hot_table = jnp.sum(
+        jnp.where(member[:, :, None, None, None], chunked[:, None], 0.0), axis=0
+    ).reshape(expert_count, chunk_rows, -1)
+    hot_total = exchange_sum(hot_table, "expert", expert_count).reshape(
+        HOT, halves, chunk_rows, -1
+    )
+    from_table = hot_total[jnp.clip(slot_rank, 0, HOT - 1)].reshape(group_sum.shape)
     d_weight = jnp.where(slot_hot[:, None, None], from_table, group_sum)[None]
     return (d_hidden, d_gate, d_weight)
 

time: 360 us -> 375 us (1.042)
  waiting for transfers between devices: 134 us -> 148 us
  other arithmetic: 11.5 us -> 16.3 us
    all_to_all x1, waiting for transfers between devices: 10.5 us -> 28.7 us  [exchange_sum(): lax.all_to_all(x.reshape(count, 8, -1), axis, split_axis=0, concat_axis=0...]
    reduce_scatter x1, waiting for transfers between devices: 60.8 us -> 56.9 us  [per_device(): lax.psum_scatter(partial_value, 'dp', scatter_dimension=1, tiled=True)]
where the time goes in v6:
time: 375 us; the launch traced here: 374 us
  waiting for transfers between devices  148 us (39%)
  blocking collectives  116 us (31%)
  local copies, waits for them, and re-layouts  36.5 us (10%)
  starting transfers between devices  23.9 us (6%)
  matrix products  18.9 us (5%)
  other arithmetic  16.3 us (4%)
  between operations  14.3 us (4%)
    all_to_all x1, blocking collectives, per_device(): lax.all_to_all(sent, 'expert', split_axis=0, concat_axis=0, tiled=True)  116 us
    reduce_scatter x1, waiting for transfers between devices, per_device(): lax.psum_scatter(partial_value, 'dp', scatter_dimension=1, tiled=True)  56.9 us
    all_to_all x1, waiting for transfers between devices, per_device(): lax.all_to_all(jnp.concatenate([back_rows, back_block], axis=-1), 'expert...  38.5 us
    all_to_all x1, waiting for transfers between devices, exchange_sum(): lax.all_to_all(x.reshape(count, 8, -1), axis, split_axis=0, concat_axis=0...  28.7 us
    all_to_all x1, waiting for transfers between devices, exchange_sum(): lax.all_to_all(copies, axis, split_axis=0, concat_axis=0, tiled=True)  23.6 us
    all_to_all x1, starting transfers between devices, exchange_sum(): lax.all_to_all(x.reshape(count, 8, -1), axis, split_axis=0, concat_axis=0...  9.78 us
    dot_general x1, matrix products, per_device(): jnp.dot(picks, block_table, preferred_element_type=jnp.float32)  8.62 us
    all_to_all x1, starting transfers between devices, per_device(): lax.all_to_all(jnp.concatenate([back_rows, back_block], axis=-1), 'expert...  7.7 us
  transfers between devices with their start and end apart: 4, of which 4 were waited for; matrix products, arithmetic and copies ran while one was open for 8% of the time, Pallas kernels for 0%

profile of v6, /device:TPU:192, one launch (start us, length us, event | category | flops | bytes accessed | tf_op | source)
XLA Modules:
  0.0 374.0 jit_solution(6800463185177425969)
XLA Ops:
  10.9 3.2 fusion.2
  14.1 2.3 fusion.20
  16.3 1.9 copy.70
  18.7 8.6 %convolution_convert_fusion = bf16[1536,1536]{1,0:T(8,128)(2,1)S(1)} fusion(bf16[1024,512]{1,0:T(8,128)(2,1)S(1)} %fusion.31, bf16[128,1024]{1,0:T(8,128)(2,1)} %param.7, bf16[1536,1024]{1,0:T(8,128)(2,1)} %fusion.2, bf16[1536,128]{1,0:T(8,128)(2,1)} %copy.70), kind=kOutput, calls=%fused_computation.3 | convolution fusion | flops 5459410944 | bytes 9568256 | tf_op jit(solution)/shard_map/dot_general | solution.py:82
  27.3 116.3 %all_to_all.20 = bf16[32,48,1536]{2,1,0:T(8,128)(2,1)S(1)} all-to-all(bf16[32,48,1536]{2,1,0:T(8,128)(2,1)S(1)} %bitcast.46), channel_id=1, replica_groups=mesh['dp'=16,'expert'=32] {'expert'}, dimensions={0} | all-to-all | bytes 9437184 | tf_op jit(solution)/shard_map/all_to_all | solution.py:86
  143.6 2.1 copy-done.1
  146.9 2.4 slice.27
  149.3 2.3 slice.28
  151.6 3.6 fusion.24
  160.1 56.9 %reduce-scatter.2.cloned.1.call-done = f32[3,24,1024]{2,1,0:T(8,128)} async-done(((f32[3,384,1024]{2,1,0:T(8,128)}), f32[3,24,1024]{2,1,0:T(8,128)}) %reduce-scatter.2.cloned.1.call-update) | async-done | bytes 294928 | tf_op jit(solution)/shard_map/reduce_scatter | solution.py:121
  217.1 1.7 broadcast_in_dim.61
  218.8 2.9 select_reduce_fusion
  221.7 9.8 %all-to-all-start.2 = ((f32[32,8,1536]{2,1,0:T(8,128)}), f32[32,8,1536]{2,1,0:T(8,128)}, u32[]{:S(2)}, u32[]{:S(2)}) async-start(f32[32,8,1536]{2,1,0:T(8,128)} %bitcast.44), calls=%async_computation.3 | async-start | bytes 3145728 | tf_op jit(solution)/shard_map/all_to_all | solution.py:34
  231.5 4.4 %fusion.22 = (bf16[32,3,16,384]{3,2,0,1:T(8,128)(2,1)S(1)}, bf16[32,3,16]{2,0,1:T(8,128)(2,1)}) fusion(f32[32,3,16]{2,0,1:T(8,128)} %copy.74, bf16[1,3,384,1024]{3,2,1,0:T(8,128)(2,1)S(1)} %copy-done, bf16[32,3,16,1024]{3,2,1,0:T(8,128)(2,1)} %bitcast.48, bf16[32,3,16,384]{3,2,1,0:T(8,128)(2,1)S(1)} %bitcast.50), kind=kOutput, calls=%fused_computation.33 | convolution fusion | flops 1210907136 | bytes 7873536 | tf_op jit(solution)/shard_map/xscd,sfd->xscf/dot_general | solution.py:94
  238.0 2.4 fusion.29
  240.4 28.7 %all-to-all-done.2 = f32[32,8,1536]{2,1,0:T(8,128)} async-done(((f32[32,8,1536]{2,1,0:T(8,128)}), f32[32,8,1536]{2,1,0:T(8,128)}, u32[]{:S(2)}, u32[]{:S(2)}) %all-to-all-start.2) | async-done | bytes 1572896 | tf_op jit(solution)/shard_map/all_to_all | solution.py:34
  269.1 7.7 %all-to-all-start.1 = ((bf16[32,48,512]{2,1,0:T(8,128)(2,1)}), bf16[32,48,512]{2,1,0:T(8,128)(2,1)}, u32[]{:S(2)}, u32[]{:S(2)}) async-start(bf16[32,48,512]{2,1,0:T(8,128)(2,1)} %fusion.29), calls=%async_computation.1 | async-start | bytes 3145728 | tf_op jit(solution)/shard_map/all_to_all | solution.py:104
  276.8 1.5 reduce_sum.79
  278.3 38.5 %all-to-all-done.1 = bf16[32,48,512]{2,1,0:T(8,128)(2,1)} async-done(((bf16[32,48,512]{2,1,0:T(8,128)(2,1)}), bf16[32,48,512]{2,1,0:T(8,128)(2,1)}, u32[]{:S(2)}, u32[]{:S(2)}) %all-to-all-start.1) | async-done | bytes 1572896 | tf_op jit(solution)/shard_map/all_to_all | solution.py:104
  318.1 6.4 %all-to-all-start.3 = ((f32[32,8,1536]{2,1,0:T(8,128)}), f32[32,8,1536]{2,1,0:T(8,128)}, u32[]{:S(2)}, u32[]{:S(2)}) async-start(f32[32,8,1536]{2,1,0:T(8,128)} %broadcast_in_dim.98), calls=%async_computation.4 | async-start | bytes 3145728 | tf_op jit(solution)/shard_map/all_to_all | solution.py:39
  327.9 5.0 %gather_fusion = bf16[1024,384]{1,0:T(8,128)(2,1)} fusion(bf16[1536,384]{1,0:T(8,128)(2,1)S(1)} %bitcast.43, s32[1024]{0:T(1024)S(1)} %broadcast_clamp_fusion), kind=kCustom, calls=%fused_computation | custom fusion | bytes 1576960 | tf_op jit(solution)/shard_map/gather | solution.py:113
  332.9 6.8 %gather_fusion.1 = bf16[1024]{0:T(1024)(128)(2,1)S(1)} fusion(bf16[1536]{0:T(1024)(128)(2,1)S(1)} %reshape_squeeze.4, s32[1024]{0:T(1024)S(1)} %broadcast_clamp_fusion), kind=kCustom, calls=%fused_computation.1 | custom fusion | bytes 8192 | tf_op jit(solution)/shard_map/gather | solution.py:116
  340.5 23.6 %all-to-all-done.3 = f32[32,8,1536]{2,1,0:T(8,128)} async-done(((f32[32,8,1536]{2,1,0:T(8,128)}), f32[32,8,1536]{2,1,0:T(8,128)}, u32[]{:S(2)}, u32[]{:S(2)}) %all-to-all-start.3) | async-done | bytes 1572896 | tf_op jit(solution)/shard_map/all_to_all | solution.py:39
  364.1 2.1 gather_fusion.2
  (63 shorter events, 18.6 us)
Async XLA Ops:
  7.2 224.3 %copy-start = (bf16[1,3,384,1024]{3,2,1,0:T(8,128)(2,1)S(1)}, bf16[1,3,384,1024]{3,2,1,0:T(8,128)(2,1)}, u32[]{:S(2)}) copy-start(bf16[1,3,384,1024]{3,2,1,0:T(8,128)(2,1)} %param.13) | copy-start | bytes 7077892
  7.2 209.9 %reduce-scatter.2.cloned.1.call-start = ((), (), s32[]{:S(2)}) async-start(), calls=%async_computation.5 | async-start | bytes 5013504 | tf_op jit(solution)/shard_map/reduce_scatter | solution.py:121
  10.9 7.4 %copy-start.6 = (bf16[128,8]{0,1:T(8,128)(2,1)S(1)}, bf16[128,8]{0,1:T(8,128)(2,1)}, u32[]{:S(2)}) copy-start(bf16[128,8]{0,1:T(8,128)(2,1)} %param.9) | copy-start | bytes 6148
  10.9 7.7 %copy-start.4 = (bf16[128,8,384]{2,1,0:T(8,128)(2,1)S(1)}, bf16[128,8,384]{2,1,0:T(8,128)(2,1)}, u32[]{:S(2)}) copy-start(bf16[128,8,384]{2,1,0:T(8,128)(2,1)} %param.8) | copy-start | bytes 2359300
  143.6 2.1 copy-start.1
  146.9 4.7 %copy-start.5 = (f32[32,3,16]{2,0,1:T(8,128)S(1)}, f32[32,3,16]{2,0,1:T(8,128)}, u32[]{:S(2)}) copy-start(f32[32,3,16]{2,0,1:T(8,128)} %copy.74) | copy-start | bytes 18436
  149.3 2.3 copy-start.2
  159.2 76.7 %copy-start.9 = (s32[3]{0:T(128)}, s32[3]{0:T(128)S(1)}, u32[]{:S(2)}) copy-start(s32[3]{0:T(128)S(1)} %select_reduce_fusion.2) | copy-start | bytes 40
  160.1 75.8 %copy-start.7 = (pred[3]{0:T(512)(128)(4,1)}, pred[3]{0:T(512)(128)(4,1)S(1)}, u32[]{:S(2)}) copy-start(pred[3]{0:T(512)(128)(4,1)S(1)} %fusion.38) | copy-start | bytes 13
  221.7 47.4 %all-to-all-start.2 = ((f32[32,8,1536]{2,1,0:T(8,128)}), f32[32,8,1536]{2,1,0:T(8,128)}, u32[]{:S(2)}, u32[]{:S(2)}) async-start(f32[32,8,1536]{2,1,0:T(8,128)} %bitcast.44), calls=%async_computation.3 | async-start | bytes 3145728 | tf_op jit(solution)/shard_map/all_to_all | solution.py:34
  269.1 47.7 %all-to-all-start.1 = ((bf16[32,48,512]{2,1,0:T(8,128)(2,1)}), bf16[32,48,512]{2,1,0:T(8,128)(2,1)}, u32[]{:S(2)}, u32[]{:S(2)}) async-start(bf16[32,48,512]{2,1,0:T(8,128)(2,1)} %fusion.29), calls=%async_computation.1 | async-start | bytes 3145728 | tf_op jit(solution)/shard_map/all_to_all | solution.py:104
  276.8 47.7 %copy-start.10 = (s32[3]{0:T(128)S(1)}, s32[3]{0:T(128)}, u32[]{:S(2)}) copy-start(s32[3]{0:T(128)} %copy-done.9) | copy-start | bytes 40
  318.1 45.9 %all-to-all-start.3 = ((f32[32,8,1536]{2,1,0:T(8,128)}), f32[32,8,1536]{2,1,0:T(8,128)}, u32[]{:S(2)}, u32[]{:S(2)}) async-start(f32[32,8,1536]{2,1,0:T(8,128)} %broadcast_in_dim.98), calls=%async_computation.4 | async-start | bytes 3145728 | tf_op jit(solution)/shard_map/all_to_all | solution.py:39
  332.9 33.3 %copy-start.3 = (f32[3,24,1024]{2,1,0:T(8,128)S(1)}, f32[3,24,1024]{2,1,0:T(8,128)}, u32[]{:S(2)}) copy-start(f32[3,24,1024]{2,1,0:T(8,128)} %reduce-scatter.2.cloned.1.call-done) | copy-start | bytes 884740
  332.9 33.4 %copy-start.8 = (pred[3]{0:T(512)(128)(4,1)S(1)}, pred[3]{0:T(512)(128)(4,1)}, u32[]{:S(2)}) copy-start(pred[3]{0:T(512)(128)(4,1)} %copy-done.7) | copy-start | bytes 13
Sparse Core Ops, SparseCore 0:
  155.4 61.6 reduce-scatter.1

commit v7 on v6

--- a/solution.py
+++ b/solution.py
@@ -32,9 +32,9 @@
 
 def exchange_sum(x, axis, count):
     pieces = lax.all_to_all(
-        x.reshape(count, 8, -1), axis, split_axis=0, concat_axis=0, tiled=True
+        x.reshape(count, 8, -1).astype(jnp.bfloat16), axis, split_axis=0, concat_axis=0, tiled=True
     )
-    own_total = jnp.sum(pieces, axis=0)
+    own_total = jnp.sum(pieces.astype(jnp.float32), axis=0)
     copies = jnp.broadcast_to(own_total[None], pieces.shape)
     totals = lax.all_to_all(copies, axis, split_axis=0, concat_axis=0, tiled=True)
     return totals.reshape(x.shape)
@@ -56,13 +56,11 @@
     spots = jnp.arange(length, dtype=jnp.int32)
     chosen = places[None, :] == spots[:, None]
     pick_route = chosen.astype(jnp.bfloat16)
-    route_token = (
-        jnp.arange(route_count, dtype=jnp.int32)[:, None] // chosen_count
-        == jnp.arange(tok_rows, dtype=jnp.int32)[None, :]
+    token_plus = jnp.arange(route_count, dtype=jnp.int32) // chosen_count + 1
+    token_of_spot = jnp.sum(jnp.where(chosen, token_plus[None, :], 0), axis=1)
+    pick_token = (
+        token_of_spot[:, None] == jnp.arange(1, tok_rows + 1, dtype=jnp.int32)[None, :]
     ).astype(jnp.bfloat16)
-    pick_token = jnp.dot(pick_route, route_token, preferred_element_type=jnp.float32).astype(
-        jnp.bfloat16
-    )
     route_table = jnp.concatenate(
         [
             hidden.reshape(route_count, hidden_width),

time: 375 us -> 354 us (0.944)
  waiting for transfers between devices: 148 us -> 131 us
    all_to_all x1, waiting for transfers between devices: 28.7 us -> 10.9 us  [exchange_sum(): lax.all_to_all(x.reshape(count, 8, -1).astype(jnp.bfloat16), axis, split_...]
  transfers between devices with their start and end apart: 4 -> 4, of which waited for: 4 -> 4; matrix products, arithmetic and copies ran while one was open for 8% -> 9% of each run, Pallas kernels for 0% -> 0%
where the time goes in v7:
time: 354 us; the launch traced here: 353 us
  waiting for transfers between devices  131 us (37%)
  blocking collectives  116 us (33%)
  local copies, waits for them, and re-layouts  35.3 us (10%)
  starting transfers between devices  24.5 us (7%)
  other arithmetic  16.2 us (5%)
  matrix products  16.1 us (5%)
  between operations  14.3 us (4%)
    all_to_all x1, blocking collectives, per_device(): lax.all_to_all(sent, 'expert', split_axis=0, concat_axis=0, tiled=True)  116 us
    reduce_scatter x1, waiting for transfers between devices, per_device(): lax.psum_scatter(partial_value, 'dp', scatter_dimension=1, tiled=True)  57 us
    all_to_all x1, waiting for transfers between devices, per_device(): lax.all_to_all(jnp.concatenate([back_rows, back_block], axis=-1), 'expert...  39.1 us
    all_to_all x1, waiting for transfers between devices, exchange_sum(): lax.all_to_all(copies, axis, split_axis=0, concat_axis=0, tiled=True)  23.6 us
    all_to_all x1, waiting for transfers between devices, exchange_sum(): lax.all_to_all(x.reshape(count, 8, -1).astype(jnp.bfloat16), axis, split_...  10.9 us
    all_to_all x1, starting transfers between devices, exchange_sum(): lax.all_to_all(x.reshape(count, 8, -1).astype(jnp.bfloat16), axis, split_...  9.66 us
    all_to_all x1, starting transfers between devices, per_device(): lax.all_to_all(jnp.concatenate([back_rows, back_block], axis=-1), 'expert...  8.41 us
    dot_general x1, matrix products, per_device(): jnp.dot(picks, block_table, preferred_element_type=jnp.float32)  8.06 us
  transfers between devices with their start and end apart: 4, of which 4 were waited for; matrix products, arithmetic and copies ran while one was open for 9% of the time, Pallas kernels for 0%

profile of v7, /device:TPU:192, one launch (start us, length us, event | category | flops | bytes accessed | tf_op | source)
XLA Modules:
  0.0 353.4 jit_solution(8619530296232168552)
XLA Ops:
  10.9 2.5 iota_compare_fusion.2
  15.5 8.1 %convolution_convert_fusion = bf16[1536,1536]{1,0:T(8,128)(2,1)S(1)} fusion(pred[1536,1024]{1,0:T(32,128)(4,1)} %iota_compare_fusion.2, pred[1536,128]{1,0:T(32,128)(4,1)S(1)} %broadcast_compare_fusion, bf16[1024,512]{1,0:T(8,128)(2,1)S(1)} %fusion.27, bf16[128,1024]{1,0:T(8,128)(2,1)} %param.7), kind=kOutput, calls=%fused_computation.3 | convolution fusion | flops 5454102528 | bytes 7798784 | tf_op jit(solution)/shard_map/dot_general | solution.py:80
  23.6 116.3 %all_to_all.20 = bf16[32,48,1536]{2,1,0:T(8,128)(2,1)S(1)} all-to-all(bf16[32,48,1536]{2,1,0:T(8,128)(2,1)S(1)} %bitcast.45), channel_id=1, replica_groups=mesh['dp'=16,'expert'=32] {'expert'}, dimensions={0} | all-to-all | bytes 9437184 | tf_op jit(solution)/shard_map/all_to_all | solution.py:84
  139.9 2.1 copy-done.1
  143.2 2.4 slice.27
  145.6 2.4 slice.28
  148.0 3.6 %fusion.20 = f32[3,384,1024]{2,1,0:T(8,128)} fusion(bf16[32,3,16,1024]{3,2,1,0:T(8,128)(2,1)S(1)} %bitcast.46, f32[32,3,16]{2,0,1:T(8,128)S(1)} %copy-done.5, bf16[32,3,16,384]{3,2,1,0:T(8,128)(2,1)S(1)} %bitcast.48), kind=kOutput, calls=%fused_computation.33 | convolution fusion | flops 1209729024 | bytes 9050112 | tf_op jit(solution)/shard_map/xscf,xscd->sfd/dot_general | solution.py:116
  153.1 1.4 reduce-window.8
  156.5 57.0 %reduce-scatter.2.cloned.1.call-done = f32[3,24,1024]{2,1,0:T(8,128)} async-done(((f32[3,384,1024]{2,1,0:T(8,128)}), f32[3,24,1024]{2,1,0:T(8,128)}) %reduce-scatter.2.cloned.1.call-update) | async-done | bytes 294928 | tf_op jit(solution)/shard_map/reduce_scatter | solution.py:119
  213.5 1.7 broadcast_in_dim.110
  215.3 2.7 select_reduce_fusion.1
  217.9 9.7 %all-to-all-start.2 = ((bf16[32,8,1536]{2,1,0:T(8,128)(2,1)}), bf16[32,8,1536]{2,1,0:T(8,128)(2,1)}, u32[]{:S(2)}, u32[]{:S(2)}) async-start(bf16[32,8,1536]{2,1,0:T(8,128)(2,1)} %bitcast.19), calls=%async_computation.3 | async-start | bytes 1572864 | tf_op jit(solution)/shard_map/all_to_all | solution.py:34
  227.6 4.4 %fusion.18 = (bf16[32,3,16,384]{3,2,0,1:T(8,128)(2,1)S(1)}, bf16[32,3,16]{2,0,1:T(8,128)(2,1)}) fusion(f32[32,3,16]{2,0,1:T(8,128)} %copy.71, bf16[1,3,384,1024]{3,2,1,0:T(8,128)(2,1)S(1)} %copy-done, bf16[32,3,16,1024]{3,2,1,0:T(8,128)(2,1)} %bitcast.47, bf16[32,3,16,384]{3,2,1,0:T(8,128)(2,1)S(1)} %bitcast.49), kind=kOutput, calls=%fused_computation.30 | convolution fusion | flops 1210907136 | bytes 7873536 | tf_op jit(solution)/shard_map/xscd,sfd->xscf/dot_general | solution.py:92
  234.1 2.4 fusion.25
  236.5 10.9 %all-to-all-done.2 = bf16[32,8,1536]{2,1,0:T(8,128)(2,1)} async-done(((bf16[32,8,1536]{2,1,0:T(8,128)(2,1)}), bf16[32,8,1536]{2,1,0:T(8,128)(2,1)}, u32[]{:S(2)}, u32[]{:S(2)}) %all-to-all-start.2) | async-done | bytes 786464 | tf_op jit(solution)/shard_map/all_to_all | solution.py:34
  247.4 8.4 %all-to-all-start.1 = ((bf16[32,48,512]{2,1,0:T(8,128)(2,1)}), bf16[32,48,512]{2,1,0:T(8,128)(2,1)}, u32[]{:S(2)}, u32[]{:S(2)}) async-start(bf16[32,48,512]{2,1,0:T(8,128)(2,1)} %fusion.25), calls=%async_computation.1 | async-start | bytes 3145728 | tf_op jit(solution)/shard_map/all_to_all | solution.py:102
  257.1 39.1 %all-to-all-done.1 = bf16[32,48,512]{2,1,0:T(8,128)(2,1)} async-done(((bf16[32,48,512]{2,1,0:T(8,128)(2,1)}), bf16[32,48,512]{2,1,0:T(8,128)(2,1)}, u32[]{:S(2)}, u32[]{:S(2)}) %all-to-all-start.1) | async-done | bytes 1572896 | tf_op jit(solution)/shard_map/all_to_all | solution.py:102
  296.1 1.3 broadcast_in_dim.113
  297.5 6.4 %all-to-all-start.3 = ((f32[32,8,1536]{2,1,0:T(8,128)}), f32[32,8,1536]{2,1,0:T(8,128)}, u32[]{:S(2)}, u32[]{:S(2)}) async-start(f32[32,8,1536]{2,1,0:T(8,128)} %broadcast_in_dim.113), calls=%async_computation.4 | async-start | bytes 3145728 | tf_op jit(solution)/shard_map/all_to_all | solution.py:39
  305.9 1.4 slice.29
  307.3 5.0 %gather_fusion = bf16[1024,384]{1,0:T(8,128)(2,1)} fusion(bf16[1536,384]{1,0:T(8,128)(2,1)S(1)} %bitcast.43, s32[1024]{0:T(1024)S(1)} %broadcast_clamp_fusion), kind=kCustom, calls=%fused_computation | custom fusion | bytes 1576960 | tf_op jit(solution)/shard_map/gather | solution.py:111
  312.3 6.8 %gather_fusion.1 = bf16[1024]{0:T(1024)(128)(2,1)S(1)} fusion(bf16[1536]{0:T(1024)(128)(2,1)S(1)} %reshape_squeeze.4, s32[1024]{0:T(1024)S(1)} %broadcast_clamp_fusion), kind=kCustom, calls=%fused_computation.1 | custom fusion | bytes 8192 | tf_op jit(solution)/shard_map/gather | solution.py:114
  319.9 23.6 %all-to-all-done.3 = f32[32,8,1536]{2,1,0:T(8,128)} async-done(((f32[32,8,1536]{2,1,0:T(8,128)}), f32[32,8,1536]{2,1,0:T(8,128)}, u32[]{:S(2)}, u32[]{:S(2)}) %all-to-all-start.3) | async-done | bytes 1572896 | tf_op jit(solution)/shard_map/all_to_all | solution.py:39
  343.5 2.1 gather_fusion.2
  (62 shorter events, 17.4 us)
Async XLA Ops:
  7.2 220.4 %copy-start = (bf16[1,3,384,1024]{3,2,1,0:T(8,128)(2,1)S(1)}, bf16[1,3,384,1024]{3,2,1,0:T(8,128)(2,1)}, u32[]{:S(2)}) copy-start(bf16[1,3,384,1024]{3,2,1,0:T(8,128)(2,1)} %param.13) | copy-start | bytes 7077892
  7.2 8.2 %copy-start.4 = (bf16[128,8,384]{2,1,0:T(8,128)(2,1)S(1)}, bf16[128,8,384]{2,1,0:T(8,128)(2,1)}, u32[]{:S(2)}) copy-start(bf16[128,8,384]{2,1,0:T(8,128)(2,1)} %param.8) | copy-start | bytes 2359300
  7.2 206.3 %reduce-scatter.2.cloned.1.call-start = ((), (), s32[]{:S(2)}) async-start(), calls=%async_computation.5 | async-start | bytes 5013504 | tf_op jit(solution)/shard_map/reduce_scatter | solution.py:119
  139.9 2.1 copy-start.1
  145.6 2.4 copy-start.2
  145.6 2.4 copy-start.5
  155.6 76.4 %copy-start.8 = (s32[3]{0:T(128)}, s32[3]{0:T(128)S(1)}, u32[]{:S(2)}) copy-start(s32[3]{0:T(128)S(1)} %select_reduce_fusion.3) | copy-start | bytes 40
  156.4 75.6 %copy-start.6 = (pred[3]{0:T(512)(128)(4,1)}, pred[3]{0:T(512)(128)(4,1)S(1)}, u32[]{:S(2)}) copy-start(pred[3]{0:T(512)(128)(4,1)S(1)} %fusion.34) | copy-start | bytes 13
  217.9 29.5 %all-to-all-start.2 = ((bf16[32,8,1536]{2,1,0:T(8,128)(2,1)}), bf16[32,8,1536]{2,1,0:T(8,128)(2,1)}, u32[]{:S(2)}, u32[]{:S(2)}) async-start(bf16[32,8,1536]{2,1,0:T(8,128)(2,1)} %bitcast.19), calls=%async_computation.3 | async-start | bytes 1572864 | tf_op jit(solution)/shard_map/all_to_all | solution.py:34
  247.4 48.8 %all-to-all-start.1 = ((bf16[32,48,512]{2,1,0:T(8,128)(2,1)}), bf16[32,48,512]{2,1,0:T(8,128)(2,1)}, u32[]{:S(2)}, u32[]{:S(2)}) async-start(bf16[32,48,512]{2,1,0:T(8,128)(2,1)} %fusion.25), calls=%async_computation.1 | async-start | bytes 3145728 | tf_op jit(solution)/shard_map/all_to_all | solution.py:102
  257.0 46.9 %copy-start.9 = (s32[3]{0:T(128)S(1)}, s32[3]{0:T(128)}, u32[]{:S(2)}) copy-start(s32[3]{0:T(128)} %copy-done.8) | copy-start | bytes 40
  297.5 46.0 %all-to-all-start.3 = ((f32[32,8,1536]{2,1,0:T(8,128)}), f32[32,8,1536]{2,1,0:T(8,128)}, u32[]{:S(2)}, u32[]{:S(2)}) async-start(f32[32,8,1536]{2,1,0:T(8,128)} %broadcast_in_dim.113), calls=%async_computation.4 | async-start | bytes 3145728 | tf_op jit(solution)/shard_map/all_to_all | solution.py:39
  312.3 33.4 %copy-start.3 = (f32[3,24,1024]{2,1,0:T(8,128)S(1)}, f32[3,24,1024]{2,1,0:T(8,128)}, u32[]{:S(2)}) copy-start(f32[3,24,1024]{2,1,0:T(8,128)} %reduce-scatter.2.cloned.1.call-done) | copy-start | bytes 884740
  312.3 33.4 %copy-start.7 = (pred[3]{0:T(512)(128)(4,1)S(1)}, pred[3]{0:T(512)(128)(4,1)}, u32[]{:S(2)}) copy-start(pred[3]{0:T(512)(128)(4,1)} %copy-done.6) | copy-start | bytes 13
Sparse Core Ops, SparseCore 0:
  151.8 61.7 reduce-scatter.1
